TPU v7x, 256 devices: a whole 4x4x8 slice. The times are simulated.
256 devices in a mesh: role: 2 (over core), dp: 16 (over x, y), tensor: 8 (over z).
Axes of the slice: x: 4, y: 4, z: 8, core: 2. Of those that a mesh axis runs over, the one named last changes fastest.
Arguments:
- queries: bfloat16 [1024, 128, 576], P(('dp', 'tensor'), 'role'), may hold values from -13 to 13
- latent_cache: bfloat16 [512, 1024, 576], P(('dp', 'tensor')), may hold values from -4 to 4
- new_latent: bfloat16 [1024, 576], P(('dp', 'tensor')), may hold values from -9 to 9
- cache_lengths: int32 [512], P(('dp', 'tensor')), may hold values from 2 to 1024
- value_proj: bfloat16 [128, 512, 128], P(('role', 'tensor')), may hold values from -1 to 1
- out_proj: bfloat16 [16384, 7168], P(('role', 'tensor'), 'dp'), may hold values from -0.046875 to 0.046875
- residual: bfloat16 [1024, 7168], P(('role', 'tensor'), 'dp'), may hold values from -68 to 68
- norm_gain: bfloat16 [7168], replicated, may hold values from 0.5 to 1.5
- routes: int32 [1024, 8], P(('role', 'tensor')), may hold values from 0 to 15, all different within a row; in each aligned block of 64 rows (0 to 63, 64 to 127, ...) at most 40 rows name the same one
- gate_values: float32 [1024, 8], P(('role', 'tensor')), may hold values from 0.2 to 0.8
- tenant_ids: int32 [1024], P(('role', 'tensor')), may hold values from 0 to 2
- expert_gate_weight: bfloat16 [16, 7168, 2048], P('dp', None, ('role', 'tensor')), may hold values from -0.0625 to 0.0625
- expert_up_weight: bfloat16 [16, 7168, 2048], P('dp', None, ('role', 'tensor')), may hold values from -0.0625 to 0.0625
- expert_down_weight: bfloat16 [16, 2048, 7168], P('dp', ('role', 'tensor')), may hold values from -0.125 to 0.125
- left_delta_factor: bfloat16 [3, 16, 2048, 64], P(None, 'dp', ('role', 'tensor')), may hold values from -0.125 to 0.125
- factor_right: bfloat16 [3, 16, 64, 7168], P(None, 'dp'), may hold values from -0.75 to 0.75
Outputs:
- mixed: bfloat16 [1024, 7168], P(('role', 'tensor'), 'dp')
Inputs may be any that keep to these rules, and one draw needn't show every extreme that they name: `routes`: in each aligned block of 64 tokens no expert is named by more than 40 of them.
All inputs are finite; a program needn't handle non-finite values.
Results may differ from a plain program's by a relative error of at most 0.008.
Values may be sent and summed in bfloat16 or wider, within the bound.
No kernel may reach another device: no remote copies, remote signals or barrier semaphores. Data moves between devices by JAX's collectives and lax.ppermute only.
A program may use at most 128 MiB of HBM per device.

v0:
```python
import jax
import jax.numpy as jnp
from jax import lax
from jax.sharding import PartitionSpec as P

LAT = 512
EXPERTS = 16
TEN = 3


SCORE_SCALE = 0.07216878364870323
NORM_EPS = 1e-06
MASKED = -1e30


def rms_rows(input_rows, norm_gain):
    wide = input_rows.astype(jnp.float32)
    scale = lax.rsqrt(jnp.mean(wide * wide, axis=-1, keepdims=True) + NORM_EPS)
    return (wide * scale * norm_gain.astype(jnp.float32)).astype(jnp.bfloat16)


def local(
    queries,
    latent_cache,
    new_latent,
    cache_lengths,
    value_proj,
    out_proj,
    residual,
    norm_gain,
    routes,
    gate_values,
    tenant_ids,
    expert_gate_weight,
    expert_up_weight,
    expert_down_weight,
    left_delta_factor,
    factor_right,
):
    seq_count, context, width = latent_cache.shape
    local_heads = queries.shape[1]
    paired = queries.reshape(seq_count, 2, local_heads, width)
    scores = (
        jnp.einsum("sqhd,spd->sqhp", paired, latent_cache, preferred_element_type=jnp.float32)
        * SCORE_SCALE
    )
    present = jnp.arange(context, dtype=jnp.int32)[None, :] < cache_lengths[:, None]
    scores = jnp.where(present[:, None, None, :], scores, MASKED)
    fresh_keys = new_latent.reshape(seq_count, 2, width)
    fresh = (
        jnp.einsum("sqhd,skd->sqhk", paired, fresh_keys, preferred_element_type=jnp.float32)
        * SCORE_SCALE
    )
    causal = jnp.arange(2)[:, None] >= jnp.arange(2)[None, :]
    fresh = jnp.where(causal[None, :, None, :], fresh, MASKED)
    top = jnp.maximum(jnp.max(scores, axis=3), jnp.max(fresh, axis=3))[..., None]
    weights = jnp.exp(scores - top)
    fresh_weights = jnp.exp(fresh - top)
    total = jnp.sum(weights, axis=3) + jnp.sum(fresh_weights, axis=3)
    summed = jnp.einsum(
        "sqhp,spd->sqhd",
        weights.astype(jnp.bfloat16),
        latent_cache[:, :, :LAT],
        preferred_element_type=jnp.float32,
    )
    summed = summed + jnp.einsum(
        "sqhk,skd->sqhd",
        fresh_weights.astype(jnp.bfloat16),
        fresh_keys[:, :, :LAT],
        preferred_element_type=jnp.float32,
    )
    attended = (
        (summed / total[..., None]).astype(jnp.bfloat16).reshape(seq_count * 2, local_heads, LAT)
    )
    by_head = lax.all_to_all(attended, "tensor", split_axis=1, concat_axis=0, tiled=True)
    head_values = jnp.einsum(
        "thl,hlv->thv", by_head, value_proj, preferred_element_type=jnp.float32
    ).astype(jnp.bfloat16)
    head_values = head_values.reshape(
        head_values.shape[0], head_values.shape[1] * head_values.shape[2]
    )
    all_values = lax.all_gather(head_values, "dp", axis=0, tiled=True)
    group_rows = residual.shape[0]
    input_rows = all_values
    attention = lax.psum_scatter(
        jnp.dot(input_rows, out_proj, preferred_element_type=jnp.float32),
        ("role", "tensor"),
        scatter_dimension=0,
        tiled=True,
    )
    mixed_in = lax.optimization_barrier(
        (residual.astype(jnp.float32) + attention).astype(jnp.bfloat16)
    )
    capacity = 5 * group_rows // 8
    labels = jnp.arange(EXPERTS, dtype=jnp.int32)
    chosen = (routes[:, :, None] == labels[None, None, :]).astype(jnp.int32)
    routed = jnp.sum(chosen, axis=1)
    earlier = jnp.cumsum(routed, axis=0) - routed
    slot_ids = jnp.arange(capacity, dtype=jnp.int32)
    table = (routed.T[:, None, :] > 0) & (earlier.T[:, None, :] == slot_ids[None, :, None])
    local_experts = EXPERTS // lax.axis_size("dp")
    expert_start = lax.axis_index("dp") * local_experts
    mine = lax.dynamic_slice_in_dim(table, expert_start, local_experts, 0)
    full_rows = lax.all_gather(mixed_in, "dp", axis=1, tiled=True)
    picked = jnp.einsum(
        "ecg,gd->ecd", mine.astype(jnp.bfloat16), full_rows, preferred_element_type=jnp.float32
    ).astype(jnp.bfloat16)
    slot_rows = rms_rows(picked, norm_gain)
    slot_owner = jnp.sum(mine.astype(jnp.int32) * tenant_ids[None, None, :], axis=2)
    collected_rows, owners = (
        lax.all_gather(slot_rows, ("role", "tensor"), axis=1, tiled=True),
        lax.all_gather(slot_owner, ("role", "tensor"), axis=1, tiled=True),
    )
    gate_scores = jnp.einsum(
        "gpc,gcb->gpb", collected_rows, expert_gate_weight, preferred_element_type=jnp.float32
    )
    upper_bound = jnp.einsum(
        "gpc,gcb->gpb", collected_rows, expert_up_weight, preferred_element_type=jnp.float32
    )
    hidden = (jax.nn.silu(gate_scores) * upper_bound).astype(jnp.bfloat16)
    owner_mask = (owners[:, :, None] == jnp.arange(TEN, dtype=jnp.int32)[None, None, :]).astype(
        jnp.float32
    )
    widened_right_factor = factor_right.astype(jnp.float32)
    input_rows = hidden
    base_output = jnp.einsum(
        "xog,xgm->oxm", input_rows, expert_down_weight, preferred_element_type=jnp.float32
    )
    mixing_coefficient = (
        jnp.einsum(
            "ywv,oyvh->ywoh", input_rows, left_delta_factor, preferred_element_type=jnp.float32
        )
        * owner_mask[..., None]
    )
    outputs = lax.psum_scatter(
        base_output
        - jnp.einsum(
            "okei,eoiw->kow",
            mixing_coefficient,
            widened_right_factor,
            precision=lax.Precision.HIGHEST,
        ),
        ("role", "tensor"),
        scatter_dimension=0,
        tiled=True,
    ).astype(jnp.bfloat16)
    gate_of = jnp.sum(gate_values[:, :, None] * chosen.astype(jnp.float32), axis=1)
    weighting = table.astype(jnp.float32) * gate_of.T[:, None, :]
    own_weights = lax.dynamic_slice_in_dim(weighting, expert_start, local_experts, 0)
    token_terms = jnp.einsum(
        "lcg,cld->gd", own_weights, outputs.astype(jnp.float32), precision=lax.Precision.HIGHEST
    )
    expert_part = lax.psum_scatter(token_terms, "dp", scatter_dimension=1, tiled=True)
    return (mixed_in.astype(jnp.float32) + expert_part).astype(jnp.bfloat16)


def solution(mesh):
    placed = (
        P(("dp", "tensor"), "role", None),
        P(("dp", "tensor"), None, None),
        P(("dp", "tensor"), None),
        P(("dp", "tensor")),
        P(("role", "tensor"), None, None),
        P(("role", "tensor"), "dp"),
        P(("role", "tensor"), "dp"),
        P(),
        P(("role", "tensor"), None),
        P(("role", "tensor"), None),
        P(("role", "tensor")),
        P("dp", None, ("role", "tensor")),
        P("dp", None, ("role", "tensor")),
        P("dp", ("role", "tensor"), None),
        P(None, "dp", ("role", "tensor"), None),
        P(None, "dp", None, None),
    )
    return jax.shard_map(
        local, mesh=mesh, in_specs=placed, out_specs=P(("role", "tensor"), "dp"), check_vma=False
    )
```

profile of v0, /device:TPU:32, one launch (start us, length us, event | category | flops | bytes accessed | tf_op | source)
XLA Modules:
  0.0 579.4 jit_solution(11137241923393458110)
XLA Ops:
  6.5 0.0 copy-start
  6.5 0.0 all-gather.6.cloned.1.call-start
  6.5 0.9 iota_compare_fusion.2
  7.4 0.7 reshape.191
  8.1 0.0 copy-start.3
  8.2 0.0 slice-start.1
  8.2 3.9 fusion.8
  12.1 0.0 copy-done.3
  12.1 0.4 fusion.59
  12.6 0.6 fusion.15
  13.2 0.0 slice-done
  13.2 0.0 slice-done.1
  13.2 0.0 copy-start.6
  13.2 2.5 fusion.4
  15.7 0.0 copy-done.6
  15.8 0.0 copy-start.2
  15.8 1.7 fusion.18
  17.5 0.3 copy.41
  17.8 24.4 %all_to_all.18 = bf16[8,64,512]{2,0,1:T(8,128)(2,1)S(1)} all-to-all(bf16[8,64,512]{2,0,1:T(8,128)(2,1)S(1)} %copy.41), channel_id=1, replica_groups=mesh['role'=2,'dp'=16,'tensor'=8] {'tensor'}, dimensions={1} | all-to-all | bytes 1048576 | tf_op jit(solution)/shard_map/all_to_all | solution.py:75
  42.2 0.3 fusion.25
  42.5 0.7 copy.61
  43.2 0.0 all-gather.6.cloned.1.call-update
  43.2 0.0 reduce-scatter.6.cloned.1.call-start
  43.3 47.3 %all-gather.6.cloned.1.call-done = bf16[1024,1024]{1,0:T(8,128)(2,1)} async-done(((bf16[64,1024]{1,0:T(8,128)(2,1)}), bf16[1024,1024]{1,0:T(8,128)(2,1)}) %all-gather.6.cloned.1.call-update) | async-done | bytes 2097168 | tf_op jit(solution)/shard_map/all_gather | solution.py:82
  90.6 4.4 fusion.60
  95.0 0.0 reduce-scatter.6.cloned.1.call-update
  95.0 0.0 all-gather.8.cloned.1.call-start
  95.1 0.6 copy-done.7
  95.7 0.1 copy.44
  95.8 0.1 reduce_window_sum.11
  95.9 0.1 copy.46
  96.0 0.1 fusion.37
  96.0 65.8 %reduce-scatter.6.cloned.1.call-done = f32[64,448]{1,0:T(8,128)} async-done(((f32[1024,448]{1,0:T(8,128)}), f32[64,448]{1,0:T(8,128)}) %reduce-scatter.6.cloned.1.call-update) | async-done | bytes 114704 | tf_op jit(solution)/shard_map/reduce_scatter | solution.py:85
  161.9 0.9 add_convert_fusion.1
  162.8 24.9 %all-gather.2 = bf16[16,448,64]{1,2,0:T(8,128)(2,1)S(1)} all-gather(bf16[1,448,64]{1,2,0:T(8,128)(2,1)S(1)} %bitcast.111), channel_id=1, replica_groups=mesh['role'=2,'dp'=16,'tensor'=8] {'dp'}, dimensions={0}, use_global_device_ids=true | all-gather | bytes 974848 | tf_op jit(solution)/shard_map/all_gather | solution.py:104
  187.7 1.6 copy.47
  189.3 2.9 reshape.187
  192.2 1.6 multiply_reduce_fusion
  193.8 1.0 multiply_convert_fusion
  194.9 0.0 all-gather.8.cloned.1.call-update
  194.9 0.0 reduce-scatter.8.cloned.1.call-start
  194.9 0.6 dynamic-slice
  196.2 0.0 copy-done.10
  196.2 0.1 select_reduce_fusion
  196.3 0.2 dynamic-update-slice
  196.6 11.9 %all-reduce = s32[640]{0:T(1024)S(1)} all-reduce(s32[640]{0:T(1024)S(1)} %dynamic-update-slice), channel_id=3, replica_groups=mesh['role'=2,'dp'=16,'tensor'=8] {'role','tensor'}, use_global_device_ids=true, to_apply=%add | all-reduce | flops 640 | bytes 5120
  208.5 41.6 %all-gather.8.cloned.1.call-done = bf16[640,7168]{1,0:T(8,128)(2,1)} async-done(((bf16[40,7168]{1,0:T(8,128)(2,1)}), bf16[640,7168]{1,0:T(8,128)(2,1)}) %all-gather.8.cloned.1.call-update) | async-done | bytes 9175056 | tf_op jit(solution)/shard_map/all_gather | solution.py:111
  250.1 6.8 %fusion.13 = f32[640,128]{1,0:T(8,128)S(1)} fusion(bf16[640,7168]{1,0:T(8,128)(2,1)} %all-gather.8.cloned.1.call-done, bf16[1,7168,128]{2,1,0:T(8,128)(2,1)} %param.27), kind=kOutput, calls=%fused_computation.18 | convolution fusion | flops 1174405120 | bytes 11337728 | tf_op jit(solution)/shard_map/gpc,gcb->gpb/dot_general | solution.py:114
  256.9 0.0 copy-done.11
  256.9 0.4 copy-done.12
  257.4 2.6 fusion.22
  259.9 0.0 copy-start.5
  259.9 8.8 %fusion.9 = f32[640,7168]{1,0:T(8,128)} fusion(bf16[640,128]{1,0:T(8,128)(2,1)S(1)} %fusion.22, bf16[1,128,7168]{2,1,0:T(8,128)(2,1)S(1)} %copy-done.1), kind=kOutput, calls=%fused_computation.14 | convolution fusion | flops 1174405120 | bytes 20348928 | tf_op jit(solution)/shard_map/xog,xgm->oxm/dot_general | solution.py:126
  268.8 0.2 fusion.61
  269.0 14.8 %fusion = f32[640,1,7168]{2,0,1:T(8,128)} fusion(f32[640,7168]{1,0:T(8,128)} %fusion.9, bf16[3,1,64,7168]{3,2,1,0:T(8,128)(2,1)S(1)} %copy-done, f32[640,3,64]{0,2,1:T(8,128)S(1)} %bitcast.107, f32[640,3]{0,1:T(4,128)S(1)} %fusion.47), kind=kOutput, calls=%fused_computation.1 | convolution fusion | flops 10574356480 | bytes 39951872 | tf_op jit(solution)/shard_map/okei,eoiw->kow/dot_general | solution.py:137
  283.8 0.0 reduce-scatter.8.cloned.1.call-update
  283.8 0.0 reduce-scatter.10.cloned.1.call-start
  283.9 0.6 copy-done.9
  284.5 198.7 %reduce-scatter.8.cloned.1.call-done = f32[40,1,7168]{2,0,1:T(8,128)} async-done(((f32[640,1,7168]{2,0,1:T(8,128)}), f32[40,1,7168]{2,0,1:T(8,128)}) %reduce-scatter.8.cloned.1.call-update) | async-done | bytes 1146896 | tf_op jit(solution)/shard_map/reduce_scatter | solution.py:135
  483.2 5.1 convolution_bitcast_fusion
  488.3 0.0 reduce-scatter.10.cloned.1.call-update
  488.3 82.9 %reduce-scatter.10.cloned.1.call-done = f32[448,64]{1,0:T(8,128)} async-done(((f32[7168,64]{1,0:T(8,128)}), f32[448,64]{1,0:T(8,128)}) %reduce-scatter.10.cloned.1.call-update) | async-done | bytes 114704
  571.1 1.0 copy.53
  572.2 0.6 add_convert_fusion
  (32 shorter events, 0.2 us)
Async XLA Ops:
  6.5 262.5 %copy-start = (bf16[3,1,64,7168]{3,2,1,0:T(8,128)(2,1)S(1)}, bf16[3,1,64,7168]{3,2,1,0:T(8,128)(2,1)}, u32[]{:S(2)}) copy-start(bf16[3,1,64,7168]{3,2,1,0:T(8,128)(2,1)} %param.31) | copy-start | bytes 8257540
  6.5 84.0 %all-gather.6.cloned.1.call-start = ((), (), s32[]{:S(2)}) async-start(), calls=%async_computation.4 | async-start | bytes 2228224 | tf_op jit(solution)/shard_map/all_gather | solution.py:82
  8.1 5.0 slice-start
  8.1 3.9 copy-start.3
  8.2 5.0 slice-start.1
  13.2 2.6 copy-start.6
  15.8 26.4 %copy-start.2 = (bf16[8,512,128]{2,1,0:T(8,128)(2,1)S(1)}, bf16[8,512,128]{2,1,0:T(8,128)(2,1)}, u32[]{:S(2)}) copy-start(bf16[8,512,128]{2,1,0:T(8,128)(2,1)} %param.20) | copy-start | bytes 3145732
  43.2 118.6 %reduce-scatter.6.cloned.1.call-start = ((), (), s32[]{:S(2)}) async-start(), calls=%async_computation.5 | async-start | bytes 2228224 | tf_op jit(solution)/shard_map/reduce_scatter | solution.py:85
  95.0 0.7 copy-start.7
  95.0 1.0 copy-start.8
  95.0 66.9 %copy-start.4 = (bf16[64,448]{1,0:T(8,128)(2,1)S(1)}, bf16[64,448]{1,0:T(8,128)(2,1)}, u32[]{:S(2)}) copy-start(bf16[64,448]{1,0:T(8,128)(2,1)} %param.22) | copy-start | bytes 172036
  95.0 155.1 %all-gather.8.cloned.1.call-start = ((), (), s32[]{:S(2)}) async-start(), calls=%async_computation.7 | async-start | bytes 9748480 | tf_op jit(solution)/shard_map/all_gather | solution.py:111
  192.2 2.7 copy-start.13
  192.2 4.0 copy-start.10
  194.9 288.3 %reduce-scatter.8.cloned.1.call-start = ((), (), s32[]{:S(2)}) async-start(), calls=%async_computation.6 | async-start | bytes 19496960 | tf_op jit(solution)/shard_map/reduce_scatter | solution.py:135
  250.1 6.8 %copy-start.11 = (bf16[640,7168]{1,0:T(8,128)(2,1)S(1)}, bf16[640,7168]{1,0:T(8,128)(2,1)}, u32[]{:S(2)}) copy-start(bf16[640,7168]{1,0:T(8,128)(2,1)} %all-gather.8.cloned.1.call-done) | copy-start | bytes 27525124
  250.1 7.2 %copy-start.12 = (bf16[1,7168,128]{2,1,0:T(8,128)(2,1)S(1)}, bf16[1,7168,128]{2,1,0:T(8,128)(2,1)}, u32[]{:S(2)}) copy-start(bf16[1,7168,128]{2,1,0:T(8,128)(2,1)} %param.28) | copy-start | bytes 5505028
  257.4 2.6 copy-start.1
  259.9 8.8 %copy-start.5 = (bf16[3,1,128,64]{2,3,1,0:T(8,128)(2,1)S(1)}, bf16[3,1,128,64]{2,3,1,0:T(8,128)(2,1)}, u32[]{:S(2)}) copy-start(bf16[3,1,128,64]{2,3,1,0:T(8,128)(2,1)} %param.30) | copy-start | bytes 147460
  283.8 0.7 copy-start.9
  283.8 287.3 %reduce-scatter.10.cloned.1.call-start = ((), (), s32[]{:S(2)}) async-start(), calls=%async_computation.8 | async-start | bytes 3899392
Sparse Core Ops, SparseCore 0:
  43.3 47.2 all-gather.5
  95.1 66.7 reduce-scatter.5
  195.0 55.0 all-gather.7
  284.0 199.1 reduce-scatter.7
  488.4 82.7 reduce-scatter.9
where the time goes:
time: 580 us; the launch traced here: 579 us
  waiting for transfers between devices  436 us (75%)
  blocking collectives  61.3 us (11%)
  matrix products  53.1 us (9%)
  between operations  14.1 us (2%)
  local copies, waits for them, and re-layouts  9.95 us (2%)
    reduce_scatter x1, waiting for transfers between devices, local(): lax.psum_scatter(base_output - jnp.einsum('okei,eoiw->kow', mixing_coeffi...  199 us
    unnamed x6, waiting for transfers between devices  83 us
    reduce_scatter x1, waiting for transfers between devices, local(): lax.psum_scatter(jnp.dot(input_rows, out_proj, preferred_element_type=jnp...  65.8 us
    all_gather x1, waiting for transfers between devices, local(): all_values = lax.all_gather(head_values, 'dp', axis=0, tiled=True)  47.3 us
    all_gather x1, waiting for transfers between devices, local(): lax.all_gather(slot_rows, ('role', 'tensor'), axis=1, tiled=True)  41.6 us
    all_gather x1, blocking collectives, local(): full_rows = lax.all_gather(mixed_in, 'dp', axis=1, tiled=True)  24.9 us
    all_to_all x1, blocking collectives, local(): lax.all_to_all(attended, 'tensor', split_axis=1, concat_axis=0, tiled=True)  24.4 us
    dot_general x1, matrix products, local(): jnp.einsum('okei,eoiw->kow', mixing_coefficient, widened_right_factor, pr...  14.8 us
  transfers between devices with their start and end apart: 5, of which 5 were waited for; matrix products, arithmetic and copies ran while one was open for 0% of the time, Pallas kernels for 0%

commit v1 on v0

v1 whole, which is shorter than its diff:
```python
import jax
import jax.numpy as jnp
from jax import lax
from jax.sharding import PartitionSpec as P

LAT = 512
EXPERTS = 16
TEN = 3


SCORE_SCALE = 0.07216878364870323
NORM_EPS = 1e-06
MASKED = -1e30
RT = ("role", "tensor")


def rms_rows(input_rows, norm_gain):
    wide = input_rows.astype(jnp.float32)
    scale = lax.rsqrt(jnp.mean(wide * wide, axis=-1, keepdims=True) + NORM_EPS)
    return (wide * scale * norm_gain.astype(jnp.float32)).astype(jnp.bfloat16)


def slot_table(routes, expert, capacity):
    hit = jnp.any(routes == expert, axis=-1).astype(jnp.int32)
    earlier = jnp.cumsum(hit, axis=-1) - hit
    slot_ids = jnp.arange(capacity, dtype=jnp.int32)
    return (hit[..., None, :] > 0) & (earlier[..., None, :] == slot_ids[:, None])


def local(
    queries,
    latent_cache,
    new_latent,
    cache_lengths,
    value_proj,
    out_proj,
    residual,
    norm_gain,
    routes,
    gate_values,
    tenant_ids,
    expert_gate_weight,
    expert_up_weight,
    expert_down_weight,
    left_delta_factor,
    factor_right,
):
    n_slices = lax.axis_size(RT)
    slice_idx = lax.axis_index(RT)
    group_rows = residual.shape[0]
    capacity = 5 * group_rows // 8
    model_width = expert_down_weight.shape[2]
    col_width = model_width // n_slices

    expert = lax.axis_index("dp")
    labels = jnp.arange(EXPERTS, dtype=jnp.int32)
    table = slot_table(routes, labels[:, None, None], capacity)
    slot_owner = jnp.sum(table.astype(jnp.int32) * tenant_ids[None, None, :], axis=2)
    lanes = 128
    all_owners = lax.all_gather(slot_owner.reshape(-1, lanes), RT, axis=0, tiled=True)
    all_owners = all_owners.reshape(n_slices, EXPERTS, capacity)
    owners = lax.dynamic_index_in_dim(all_owners, expert, 1, keepdims=False)
    owners = owners.reshape(n_slices * capacity)
    down_w = expert_down_weight[0].reshape(expert_down_weight.shape[1], n_slices, col_width)
    down_w = lax.all_to_all(down_w, RT, split_axis=1, concat_axis=0, tiled=True)
    down_w = down_w.reshape(-1, col_width)
    left_local = left_delta_factor[:, 0]
    tenants, hidden_slice, rank = left_local.shape
    left_w = lax.all_gather(left_local.reshape(-1, lanes), RT, axis=0, tiled=True)
    left_w = left_w.reshape(n_slices, tenants, hidden_slice, rank)
    left_w = jnp.transpose(left_w, (1, 0, 2, 3)).reshape(tenants, n_slices * hidden_slice, rank)
    right_w = lax.dynamic_slice_in_dim(factor_right[:, 0], slice_idx * col_width, col_width, 2)

    seq_count, context, width = latent_cache.shape
    local_heads = queries.shape[1]
    paired = queries.reshape(seq_count, 2, local_heads, width)
    scores = (
        jnp.einsum("sqhd,spd->sqhp", paired, latent_cache, preferred_element_type=jnp.float32)
        * SCORE_SCALE
    )
    present = jnp.arange(context, dtype=jnp.int32)[None, :] < cache_lengths[:, None]
    scores = jnp.where(present[:, None, None, :], scores, MASKED)
    fresh_keys = new_latent.reshape(seq_count, 2, width)
    fresh = (
        jnp.einsum("sqhd,skd->sqhk", paired, fresh_keys, preferred_element_type=jnp.float32)
        * SCORE_SCALE
    )
    causal = jnp.arange(2)[:, None] >= jnp.arange(2)[None, :]
    fresh = jnp.where(causal[None, :, None, :], fresh, MASKED)
    top = jnp.maximum(jnp.max(scores, axis=3), jnp.max(fresh, axis=3))[..., None]
    weights = jnp.exp(scores - top)
    fresh_weights = jnp.exp(fresh - top)
    total = jnp.sum(weights, axis=3) + jnp.sum(fresh_weights, axis=3)
    summed = jnp.einsum(
        "sqhp,spd->sqhd",
        weights.astype(jnp.bfloat16),
        latent_cache[:, :, :LAT],
        preferred_element_type=jnp.float32,
    )
    summed = summed + jnp.einsum(
        "sqhk,skd->sqhd",
        fresh_weights.astype(jnp.bfloat16),
        fresh_keys[:, :, :LAT],
        preferred_element_type=jnp.float32,
    )
    attended = (
        (summed / total[..., None]).astype(jnp.bfloat16).reshape(seq_count * 2, local_heads, LAT)
    )
    by_head = lax.all_to_all(attended, "tensor", split_axis=1, concat_axis=0, tiled=True)
    head_values = jnp.einsum(
        "thl,hlv->thv", by_head, value_proj, preferred_element_type=jnp.float32
    ).astype(jnp.bfloat16)
    head_values = head_values.reshape(
        head_values.shape[0], head_values.shape[1] * head_values.shape[2]
    )
    all_values = lax.all_gather(head_values, "dp", axis=0, tiled=True)
    attention = lax.psum_scatter(
        jnp.dot(all_values, out_proj, preferred_element_type=jnp.float32),
        RT,
        scatter_dimension=0,
        tiled=True,
    )
    mixed_in = lax.optimization_barrier(
        (residual.astype(jnp.float32) + attention).astype(jnp.bfloat16)
    )

    full_rows = lax.all_gather(mixed_in.reshape(-1, lanes), "dp", axis=0, tiled=True)
    full_rows = full_rows.reshape(-1, group_rows, mixed_in.shape[1])
    full_rows = jnp.transpose(full_rows, (1, 0, 2)).reshape(group_rows, model_width)
    normed = rms_rows(full_rows, norm_gain)
    mine = lax.dynamic_index_in_dim(table, expert, 0, keepdims=False)
    picked = jnp.dot(
        mine.astype(jnp.bfloat16), normed, preferred_element_type=jnp.float32
    ).astype(jnp.bfloat16)
    collected_rows = lax.all_gather(picked, RT, axis=0, tiled=True)
    gate_scores = jnp.dot(collected_rows, expert_gate_weight[0], preferred_element_type=jnp.float32)
    upper_bound = jnp.dot(collected_rows, expert_up_weight[0], preferred_element_type=jnp.float32)
    hidden = (jax.nn.silu(gate_scores) * upper_bound).astype(jnp.bfloat16)

    hidden_all = lax.all_gather(hidden, RT, axis=0, tiled=False)
    hidden_all = jnp.transpose(hidden_all, (1, 0, 2)).reshape(hidden.shape[0], -1)
    base_output = jnp.dot(hidden_all, down_w, preferred_element_type=jnp.float32)
    owner_mask = (owners[:, None] == jnp.arange(TEN, dtype=jnp.int32)[None, :]).astype(jnp.float32)
    mixing = jnp.einsum(
        "sf,tfr->str", hidden_all, left_w, preferred_element_type=jnp.float32
    ) * owner_mask[:, :, None]
    delta = jnp.einsum(
        "str,trd->sd", mixing, right_w.astype(jnp.float32), precision=lax.Precision.HIGHEST
    )
    expert_out = (base_output - delta).astype(jnp.bfloat16)
    expert_out = expert_out.reshape(n_slices, capacity, col_width)
    by_group = lax.all_to_all(expert_out, RT, split_axis=0, concat_axis=0, tiled=True)
    by_expert = lax.all_to_all(by_group, "dp", split_axis=0, concat_axis=0, tiled=True)

    chosen = (routes[:, :, None] == labels[None, None, :]).astype(jnp.float32)
    gate_of = jnp.sum(gate_values[:, :, None] * chosen, axis=1)
    weighting = table.astype(jnp.float32) * gate_of.T[:, None, :]
    expert_part = jnp.einsum(
        "ecg,ecd->gd", weighting, by_expert.astype(jnp.float32), precision=lax.Precision.HIGHEST
    )
    return (mixed_in.astype(jnp.float32) + expert_part).astype(jnp.bfloat16)


def solution(mesh):
    placed = (
        P(("dp", "tensor"), "role", None),
        P(("dp", "tensor"), None, None),
        P(("dp", "tensor"), None),
        P(("dp", "tensor")),
        P(("role", "tensor"), None, None),
        P(("role", "tensor"), "dp"),
        P(("role", "tensor"), "dp"),
        P(),
        P(("role", "tensor"), None),
        P(("role", "tensor"), None),
        P(("role", "tensor")),
        P("dp", None, ("role", "tensor")),
        P("dp", None, ("role", "tensor")),
        P("dp", ("role", "tensor"), None),
        P(None, "dp", ("role", "tensor"), None),
        P(None, "dp", None, None),
    )
    return jax.shard_map(
        local, mesh=mesh, in_specs=placed, out_specs=P(("role", "tensor"), "dp"), check_vma=False
    )
```

time: 580 us -> 462 us (0.80)
  waiting for transfers between devices: 436 us -> 181 us
  blocking collectives: 61.3 us -> 185 us
  matrix products: 53.1 us -> 33.3 us
  local copies, waits for them, and re-layouts: 9.95 us -> 28.5 us
  starting transfers between devices: 0.17 us -> 13.8 us
    reduce_scatter x2 -> x1, waiting for transfers between devices: 265 us -> 66 us  [local(): lax.psum_scatter(jnp.dot(all_values, out_proj, preferred_element_type=jnp...]
    all_gather x1 -> x3, blocking collectives: 24.9 us -> 135 us  [the longest x1 75.4 us: local(): lax.all_gather(slot_owner.reshape(-1, lanes), RT, axis=0, tiled=True)]
    unnamed x6 -> x4, waiting for transfers between devices: 83 us -> 0.07 us
    all_to_all x0 -> x1, blocking collectives: none -> 26.1 us  [local(): lax.all_to_all(expert_out, RT, split_axis=0, concat_axis=0, tiled=True)]
    dot_general x6 -> x8, matrix products: 38.9 us -> 24.5 us  [the longest x1 6.78 us: local(): jnp.dot(collected_rows, expert_gate_weight[0], preferred_element_type=jnp...]
    all_to_all x0 -> x2, starting transfers between devices: none -> 13.5 us  [the longest x1 6.81 us: local(): lax.all_to_all(by_group, 'dp', split_axis=0, concat_axis=0, tiled=True)]
    all_gather x1 -> x2, waiting for transfers between devices: 41.6 us -> 54.9 us  [the longest x1 54.9 us: local(): collected_rows = lax.all_gather(picked, RT, axis=0, tiled=True)]
    all_to_all x0 -> x2, waiting for transfers between devices: none -> 12.1 us  [the longest x1 12.1 us: local(): lax.all_to_all(by_group, 'dp', split_axis=0, concat_axis=0, tiled=True)]
  transfers between devices with their start and end apart: 5 -> 6, of which waited for: 5 -> 4; matrix products, arithmetic and copies ran while one was open for 0% -> 3% of each run, Pallas kernels for 0% -> 0%
where the time goes in v1:
time: 462 us; the launch traced here: 461 us
  blocking collectives  185 us (40%)
  waiting for transfers between devices  181 us (39%)
  matrix products  33.3 us (7%)
  local copies, waits for them, and re-layouts  28.5 us (6%)
  starting transfers between devices  13.8 us (3%)
  between operations  13.5 us (3%)
  other arithmetic  6.21 us (1%)
    all_gather x1, blocking collectives, local(): lax.all_gather(slot_owner.reshape(-1, lanes), RT, axis=0, tiled=True)  75.4 us
    reduce_scatter x1, waiting for transfers between devices, local(): lax.psum_scatter(jnp.dot(all_values, out_proj, preferred_element_type=jnp...  66 us
    all_gather x1, waiting for transfers between devices, local(): collected_rows = lax.all_gather(picked, RT, axis=0, tiled=True)  54.9 us
    all_gather x1, waiting for transfers between devices, local(): all_values = lax.all_gather(head_values, 'dp', axis=0, tiled=True)  47.3 us
    all_gather x1, blocking collectives, local(): lax.all_gather(left_local.reshape(-1, lanes), RT, axis=0, tiled=True)  33.2 us
    all_gather x1, blocking collectives, local(): lax.all_gather(mixed_in.reshape(-1, lanes), 'dp', axis=0, tiled=True)  26.3 us
    all_to_all x1, blocking collectives, local(): lax.all_to_all(expert_out, RT, split_axis=0, concat_axis=0, tiled=True)  26.1 us
    all_to_all x1, blocking collectives, local(): lax.all_to_all(attended, 'tensor', split_axis=1, concat_axis=0, tiled=True)  24.4 us
  transfers between devices with their start and end apart: 6, of which 4 were waited for; matrix products, arithmetic and copies ran while one was open for 3% of the time, Pallas kernels for 0%

profile of v1, /device:TPU:32, one launch (start us, length us, event | category | flops | bytes accessed | tf_op | source)
XLA Modules:
  0.0 461.4 jit_solution(8840428006938721950)
XLA Ops:
  6.5 0.9 iota_compare_fusion.3
  7.4 0.7 reshape.166
  8.1 0.0 copy-start.4
  8.2 3.9 fusion.5
  12.1 0.4 fusion.60
  12.6 0.6 fusion.13
  13.2 2.5 fusion.2
  15.8 1.7 fusion.18
  17.5 0.3 copy.62
  17.8 24.4 %all_to_all.43 = bf16[8,64,512]{2,0,1:T(8,128)(2,1)S(1)} all-to-all(bf16[8,64,512]{2,0,1:T(8,128)(2,1)S(1)} %copy.62), channel_id=1, replica_groups=mesh['role'=2,'dp'=16,'tensor'=8] {'tensor'}, dimensions={1} | all-to-all | bytes 1048576 | tf_op jit(solution)/shard_map/all_to_all | solution.py:109
  42.2 0.3 fusion.27
  42.5 0.7 copy.89
  43.2 0.0 all-gather.6.cloned.1.call-update
  43.2 0.0 reduce-scatter.2.cloned.1.call-start
  43.2 47.3 %all-gather.6.cloned.1.call-done = bf16[1024,1024]{1,0:T(8,128)(2,1)} async-done(((bf16[64,1024]{1,0:T(8,128)(2,1)}), bf16[1024,1024]{1,0:T(8,128)(2,1)}) %all-gather.6.cloned.1.call-update) | async-done | bytes 2097168 | tf_op jit(solution)/shard_map/all_gather | solution.py:116
  90.6 4.4 fusion.61
  95.0 0.0 reduce-scatter.2.cloned.1.call-update
  95.0 0.0 all-gather.8.cloned.1.call-start
  95.0 0.6 copy-done.12
  95.7 0.1 reshape.159
  95.8 0.2 reduce_window_sum.11
  96.0 0.1 fusion.40
  96.1 66.0 %reduce-scatter.2.cloned.1.call-done = f32[64,448]{1,0:T(8,128)} async-done(((f32[1024,448]{1,0:T(8,128)}), f32[64,448]{1,0:T(8,128)}) %reduce-scatter.2.cloned.1.call-update) | async-done | bytes 114704 | tf_op jit(solution)/shard_map/reduce_scatter | solution.py:117
  162.1 0.9 add_convert_fusion
  163.1 0.0 copy-start.5
  163.1 0.1 reshape.151
  163.2 26.3 %all_gather.22 = bf16[3584,128]{1,0:T(8,128)(2,1)} all-gather(bf16[224,128]{1,0:T(8,128)(2,1)S(1)} %reshape.151), channel_id=1, replica_groups=mesh['role'=2,'dp'=16,'tensor'=8] {'dp'}, dimensions={0}, use_global_device_ids=true | all-gather | bytes 974848 | tf_op jit(solution)/shard_map/all_gather | solution.py:127
  189.5 2.8 reshape.158
  192.4 2.1 multiply_reduce_fusion
  194.5 0.1 copy-done.1
  194.6 0.4 fusion.31
  195.0 1.5 copy.65
  196.5 2.9 convert_element_type.95
  199.5 2.3 convolution_convert_fusion
  201.8 0.0 all-gather.8.cloned.1.call-update
  201.8 0.2 all-gather.10.cloned.1.call-start
  202.0 54.9 %all-gather.8.cloned.1.call-done = bf16[640,7168]{1,0:T(8,128)(2,1)} async-done(((bf16[40,7168]{1,0:T(8,128)(2,1)}), bf16[640,7168]{1,0:T(8,128)(2,1)}) %all-gather.8.cloned.1.call-update) | async-done | bytes 9175056 | tf_op jit(solution)/shard_map/all_gather | solution.py:135
  257.0 6.8 %fusion.11 = f32[640,128]{1,0:T(8,128)S(1)} fusion(bf16[640,7168]{1,0:T(8,128)(2,1)} %all-gather.8.cloned.1.call-done, bf16[1,7168,128]{2,1,0:T(8,128)(2,1)} %param.27), kind=kOutput, calls=%fused_computation.16 | convolution fusion | flops 1174405120 | bytes 11337728 | tf_op jit(solution)/shard_map/dot_general | solution.py:136
  263.8 0.4 copy-done.17
  264.2 3.2 fusion.23
  267.4 0.0 all-gather.10.cloned.1.call-update
  267.4 3.9 copy.67
  271.3 6.7 %all-to-all-start.1 = ((bf16[128,16,448]{0,2,1:T(8,128)(2,1)}), bf16[128,16,448]{0,2,1:T(8,128)(2,1)}, u32[]{:S(2)}, u32[]{:S(2)}) async-start(bf16[128,16,448]{0,2,1:T(8,128)(2,1)} %bitcast.110), calls=%async_computation.2 | async-start | bytes 3670016 | tf_op jit(solution)/shard_map/all_to_all | solution.py:65
  278.0 0.3 select_reduce_fusion
  278.4 0.1 reshape.161
  278.5 75.4 %all-gather.1 = s32[16,5,128]{2,1,0:T(8,128)S(1)} all-gather(s32[1,5,128]{2,1,0:T(8,128)S(1)} %reshape.161), channel_id=1, replica_groups=mesh['role'=2,'dp'=16,'tensor'=8] {'role','tensor'}, dimensions={0}, use_global_device_ids=true | all-gather | bytes 43520 | tf_op jit(solution)/shard_map/all_gather | solution.py:60
  353.9 0.1 reshape.156
  354.0 0.1 eq.67
  354.1 0.1 copy.69
  354.2 0.7 reshape_squeeze.7
  355.0 33.2 %all_gather.26 = bf16[3072,128]{1,0:T(8,128)(2,1)S(1)} all-gather(bf16[192,128]{1,0:T(8,128)(2,1)} %reshape_squeeze.7), channel_id=1, replica_groups=mesh['role'=2,'dp'=16,'tensor'=8] {'role','tensor'}, dimensions={0}, use_global_device_ids=true | all-gather | bytes 835584 | tf_op jit(solution)/shard_map/all_gather | solution.py:69
  388.2 1.6 reshape.154
  389.8 1.8 copy.70
  391.6 0.6 fusion.49
  392.2 4.0 copy.68
  396.1 4.4 copy.66
  400.5 4.0 fusion.6
  404.6 1.0 fusion.19
  405.6 1.7 fusion.17
  407.3 1.3 copy.71
  408.6 26.1 %all_to_all.44 = bf16[16,40,448]{2,1,0:T(8,128)(2,1)} all-to-all(bf16[16,40,448]{2,1,0:T(8,128)(2,1)S(1)} %bitcast.116), channel_id=1, replica_groups=mesh['role'=2,'dp'=16,'tensor'=8] {'role','tensor'}, dimensions={0} | all-to-all | bytes 1146880 | tf_op jit(solution)/shard_map/all_to_all | solution.py:152
  434.7 6.8 %all-to-all-start.3 = ((bf16[16,40,448]{2,1,0:T(8,128)(2,1)}), bf16[16,40,448]{2,1,0:T(8,128)(2,1)S(1)}, u32[]{:S(2)}, u32[]{:S(2)}) async-start(bf16[16,40,448]{2,1,0:T(8,128)(2,1)} %all_to_all.44), calls=%async_computation.4 | async-start | bytes 1310720 | tf_op jit(solution)/shard_map/all_to_all | solution.py:153
  441.6 12.1 %all-to-all-done.3 = bf16[16,40,448]{2,1,0:T(8,128)(2,1)S(1)} async-done(((bf16[16,40,448]{2,1,0:T(8,128)(2,1)}), bf16[16,40,448]{2,1,0:T(8,128)(2,1)S(1)}, u32[]{:S(2)}, u32[]{:S(2)}) %all-to-all-start.3) | async-done | bytes 573472 | tf_op jit(solution)/shard_map/all_to_all | solution.py:153
  453.7 1.1 fusion.28
  (50 shorter events, 0.2 us)
Async XLA Ops:
  6.5 399.1 %copy-start = (bf16[3,1,64,7168]{3,2,1,0:T(8,128)(2,1)S(1)}, bf16[3,1,64,7168]{3,2,1,0:T(8,128)(2,1)}, u32[]{:S(2)}) copy-start(bf16[3,1,64,7168]{3,2,1,0:T(8,128)(2,1)} %param.31) | copy-start | bytes 8257540
  6.5 84.0 %all-gather.6.cloned.1.call-start = ((), (), s32[]{:S(2)}) async-start(), calls=%async_computation.5 | async-start | bytes 2228224 | tf_op jit(solution)/shard_map/all_gather | solution.py:116
  8.1 5.0 %slice-start = ((s8[4718592]{0:T(1024)(128)(4,1)}), s8[4194304]{0:T(1024)(128)(4,1)S(1)}, s32[]{:S(2)}) async-start(s8[4718592]{0:T(1024)(128)(4,1)} %bitcast.111), calls=%async_computation.9 | async-start | bytes 8388608
  8.1 3.9 copy-start.4
  8.2 5.0 %slice-start.1 = ((s8[4718592]{0:T(1024)(128)(4,1)}), s8[524288]{0:T(1024)(128)(4,1)S(1)}, s32[]{:S(2)}) async-start(s8[4718592]{0:T(1024)(128)(4,1)} %bitcast.111), calls=%async_computation.10 | async-start | bytes 1048576
  13.2 2.5 copy-start.9
  15.8 26.4 %copy-start.3 = (bf16[8,512,128]{2,1,0:T(8,128)(2,1)S(1)}, bf16[8,512,128]{2,1,0:T(8,128)(2,1)}, u32[]{:S(2)}) copy-start(bf16[8,512,128]{2,1,0:T(8,128)(2,1)} %param.20) | copy-start | bytes 3145732
  43.2 118.9 %reduce-scatter.2.cloned.1.call-start = ((), (), s32[]{:S(2)}) async-start(), calls=%async_computation.6 | async-start | bytes 2228224 | tf_op jit(solution)/shard_map/reduce_scatter | solution.py:117
  94.9 0.7 copy-start.12
  95.0 0.8 copy-start.10
  95.0 67.2 %copy-start.7 = (bf16[64,448]{1,0:T(8,128)(2,1)S(1)}, bf16[64,448]{1,0:T(8,128)(2,1)}, u32[]{:S(2)}) copy-start(bf16[64,448]{1,0:T(8,128)(2,1)} %param.22) | copy-start | bytes 172036
  95.0 162.0 %all-gather.8.cloned.1.call-start = ((), (), s32[]{:S(2)}) async-start(), calls=%async_computation.7 | async-start | bytes 9748480 | tf_op jit(solution)/shard_map/all_gather | solution.py:135
  163.1 31.4 %copy-start.5 = (bf16[64,448]{1,0:T(8,128)(2,1)}, bf16[64,448]{1,0:T(8,128)(2,1)S(1)}, u32[]{:S(2)}) copy-start(bf16[64,448]{1,0:T(8,128)(2,1)S(1)} %add_convert_fusion) | copy-start | bytes 172036
  192.4 2.2 copy-start.1
  201.8 194.3 %all-gather.10.cloned.1.call-start = ((), (), s32[]{:S(2)}) async-start(), calls=%async_computation.8 | async-start | bytes 2785280 | tf_op jit(solution)/shard_map/all_gather | solution.py:140
  257.0 6.8 %copy-start.16 = (bf16[640,7168]{1,0:T(8,128)(2,1)S(1)}, bf16[640,7168]{1,0:T(8,128)(2,1)}, u32[]{:S(2)}) copy-start(bf16[640,7168]{1,0:T(8,128)(2,1)} %all-gather.8.cloned.1.call-done) | copy-start | bytes 27525124
  257.0 7.2 %copy-start.17 = (bf16[1,7168,128]{2,1,0:T(8,128)(2,1)S(1)}, bf16[1,7168,128]{2,1,0:T(8,128)(2,1)}, u32[]{:S(2)}) copy-start(bf16[1,7168,128]{2,1,0:T(8,128)(2,1)} %param.28) | copy-start | bytes 5505028
  271.3 6.7 %copy-start.15 = (s32[64]{0:T(128)S(1)}, s32[64]{0:T(128)}, u32[]{:S(2)}) copy-start(s32[64]{0:T(128)} %param.26) | copy-start | bytes 772
  271.3 82.8 %copy-start.8 = (bf16[3,1,128,64]{2,3,1,0:T(8,128)(2,1)S(1)}, bf16[3,1,128,64]{2,3,1,0:T(8,128)(2,1)}, u32[]{:S(2)}) copy-start(bf16[3,1,128,64]{2,3,1,0:T(8,128)(2,1)} %param.30) | copy-start | bytes 147460
  271.3 120.9 %all-to-all-start.1 = ((bf16[128,16,448]{0,2,1:T(8,128)(2,1)}), bf16[128,16,448]{0,2,1:T(8,128)(2,1)}, u32[]{:S(2)}, u32[]{:S(2)}) async-start(bf16[128,16,448]{0,2,1:T(8,128)(2,1)} %bitcast.110), calls=%async_computation.2 | async-start | bytes 3670016 | tf_op jit(solution)/shard_map/all_to_all | solution.py:65
  400.5 4.0 copy-start.2
  400.5 4.0 copy-start.13
  407.3 34.3 %copy-start.11 = (s32[64,8]{0,1:T(8,128)S(1)}, s32[64,8]{0,1:T(8,128)}, u32[]{:S(2)}) copy-start(s32[64,8]{0,1:T(8,128)} %param.24) | copy-start | bytes 6148
  407.3 34.3 %copy-start.14 = (f32[64,8]{0,1:T(8,128)S(1)}, f32[64,8]{0,1:T(8,128)}, u32[]{:S(2)}) copy-start(f32[64,8]{0,1:T(8,128)} %param.25) | copy-start | bytes 6148
  407.3 46.5 %copy-start.6 = (bf16[64,448]{1,0:T(8,128)(2,1)S(1)}, bf16[64,448]{1,0:T(8,128)(2,1)}, u32[]{:S(2)}) copy-start(bf16[64,448]{1,0:T(8,128)(2,1)} %copy-done.5) | copy-start | bytes 172036
  434.7 19.0 %all-to-all-start.3 = ((bf16[16,40,448]{2,1,0:T(8,128)(2,1)}), bf16[16,40,448]{2,1,0:T(8,128)(2,1)S(1)}, u32[]{:S(2)}, u32[]{:S(2)}) async-start(bf16[16,40,448]{2,1,0:T(8,128)(2,1)} %all_to_all.44), calls=%async_computation.4 | async-start | bytes 1310720 | tf_op jit(solution)/shard_map/all_to_all | solution.py:153
Sparse Core Ops, SparseCore 0:
  43.3 47.2 all-gather.5
  95.1 66.9 reduce-scatter.1
  201.9 55.0 all-gather.7
  267.5 64.8 all-gather.9

commit v2 on v1

--- a/solution.py
+++ b/solution.py
@@ -55,20 +55,16 @@
     expert = lax.axis_index("dp")
     labels = jnp.arange(EXPERTS, dtype=jnp.int32)
     table = slot_table(routes, labels[:, None, None], capacity)
-    slot_owner = jnp.sum(table.astype(jnp.int32) * tenant_ids[None, None, :], axis=2)
-    lanes = 128
-    all_owners = lax.all_gather(slot_owner.reshape(-1, lanes), RT, axis=0, tiled=True)
-    all_owners = all_owners.reshape(n_slices, EXPERTS, capacity)
-    owners = lax.dynamic_index_in_dim(all_owners, expert, 1, keepdims=False)
-    owners = owners.reshape(n_slices * capacity)
-    down_w = expert_down_weight[0].reshape(expert_down_weight.shape[1], n_slices, col_width)
-    down_w = lax.all_to_all(down_w, RT, split_axis=1, concat_axis=0, tiled=True)
-    down_w = down_w.reshape(-1, col_width)
+    mine = lax.dynamic_index_in_dim(table, expert, 0, keepdims=False)
+    mine_owner = jnp.sum(mine.astype(jnp.int32) * tenant_ids[None, :], axis=1)
+    hidden_slice = expert_down_weight.shape[1]
+    down_local = expert_down_weight[0].reshape(hidden_slice, n_slices, col_width)
     left_local = left_delta_factor[:, 0]
-    tenants, hidden_slice, rank = left_local.shape
-    left_w = lax.all_gather(left_local.reshape(-1, lanes), RT, axis=0, tiled=True)
-    left_w = left_w.reshape(n_slices, tenants, hidden_slice, rank)
-    left_w = jnp.transpose(left_w, (1, 0, 2, 3)).reshape(tenants, n_slices * hidden_slice, rank)
+    tenants, _, rank = left_local.shape
+    left_local = jnp.transpose(left_local, (1, 0, 2)).reshape(hidden_slice, 1, tenants * rank)
+    left_local = jnp.broadcast_to(left_local, (hidden_slice, n_slices, tenants * rank))
+    down_pack = jnp.concatenate([down_local, left_local], axis=2)
+    down_pack = lax.all_to_all(down_pack, RT, split_axis=1, concat_axis=0, tiled=True)
     right_w = lax.dynamic_slice_in_dim(factor_right[:, 0], slice_idx * col_width, col_width, 2)
 
     seq_count, context, width = latent_cache.shape
@@ -114,21 +110,18 @@
         head_values.shape[0], head_values.shape[1] * head_values.shape[2]
     )
     all_values = lax.all_gather(head_values, "dp", axis=0, tiled=True)
-    attention = lax.psum_scatter(
-        jnp.dot(all_values, out_proj, preferred_element_type=jnp.float32),
-        RT,
-        scatter_dimension=0,
-        tiled=True,
-    )
+    down_pack, all_values = lax.optimization_barrier((down_pack, all_values))
+    partial = jnp.dot(all_values, out_proj, preferred_element_type=jnp.float32)
+    partial = lax.psum_scatter(partial, "role", scatter_dimension=0, tiled=True)
+    attention = lax.psum_scatter(partial, "tensor", scatter_dimension=0, tiled=True)
     mixed_in = lax.optimization_barrier(
         (residual.astype(jnp.float32) + attention).astype(jnp.bfloat16)
     )
 
-    full_rows = lax.all_gather(mixed_in.reshape(-1, lanes), "dp", axis=0, tiled=True)
+    full_rows = lax.all_gather(mixed_in.reshape(-1, 128), "dp", axis=0, tiled=True)
     full_rows = full_rows.reshape(-1, group_rows, mixed_in.shape[1])
     full_rows = jnp.transpose(full_rows, (1, 0, 2)).reshape(group_rows, model_width)
     normed = rms_rows(full_rows, norm_gain)
-    mine = lax.dynamic_index_in_dim(table, expert, 0, keepdims=False)
     picked = jnp.dot(
         mine.astype(jnp.bfloat16), normed, preferred_element_type=jnp.float32
     ).astype(jnp.bfloat16)
@@ -137,12 +130,21 @@
     upper_bound = jnp.dot(collected_rows, expert_up_weight[0], preferred_element_type=jnp.float32)
     hidden = (jax.nn.silu(gate_scores) * upper_bound).astype(jnp.bfloat16)
 
-    hidden_all = lax.all_gather(hidden, RT, axis=0, tiled=False)
-    hidden_all = jnp.transpose(hidden_all, (1, 0, 2)).reshape(hidden.shape[0], -1)
+    lanes = hidden.shape[1]
+    owner_block = jnp.zeros((8, lanes), jnp.bfloat16)
+    owner_block = owner_block.at[0, :capacity].set(mine_owner.astype(jnp.bfloat16))
+    hidden_ext = jnp.concatenate([hidden, owner_block], axis=0)
+    gathered = lax.all_gather(hidden_ext, RT, axis=0, tiled=True)
+    gathered = gathered.reshape(n_slices, hidden.shape[0] + 8, lanes)
+    owners = gathered[:, hidden.shape[0], :capacity].astype(jnp.int32).reshape(n_slices * capacity)
+    hidden_all = jnp.transpose(gathered[:, : hidden.shape[0]], (1, 0, 2)).reshape(hidden.shape[0], -1)
+    down_pack = down_pack.reshape(n_slices * hidden_slice, col_width + tenants * rank)
+    down_w = down_pack[:, :col_width]
+    left_w = down_pack[:, col_width:].reshape(n_slices * hidden_slice, tenants, rank)
     base_output = jnp.dot(hidden_all, down_w, preferred_element_type=jnp.float32)
     owner_mask = (owners[:, None] == jnp.arange(TEN, dtype=jnp.int32)[None, :]).astype(jnp.float32)
     mixing = jnp.einsum(
-        "sf,tfr->str", hidden_all, left_w, preferred_element_type=jnp.float32
+        "sf,ftr->str", hidden_all, left_w, preferred_element_type=jnp.float32
     ) * owner_mask[:, :, None]
     delta = jnp.einsum(
         "str,trd->sd", mixing, right_w.astype(jnp.float32), precision=lax.Precision.HIGHEST

time: 462 us -> 393 us (0.85)
  blocking collectives: 185 us -> 50.9 us
  waiting for transfers between devices: 181 us -> 227 us
  starting transfers between devices: 13.8 us -> 21.4 us
  other arithmetic: 6.21 us -> 12 us
    all_gather x3 -> x1, blocking collectives: 135 us -> 26.3 us  [local(): lax.all_gather(mixed_in.reshape(-1, 128), 'dp', axis=0, tiled=True)]
    all_to_all x1 -> x2, waiting for transfers between devices: 0.01 us -> 66.2 us  [the longest x1 57.4 us: local(): lax.all_to_all(down_pack, RT, split_axis=1, concat_axis=0, tiled=True)]
    all_gather x1, waiting for transfers between devices: 47.3 us -> 0.01 us  [local(): all_values = lax.all_gather(head_values, 'dp', axis=0, tiled=True)]
    all_gather x1, waiting for transfers between devices: 0.01 us -> 40.4 us  [local(): gathered = lax.all_gather(hidden_ext, RT, axis=0, tiled=True)]
    all_to_all x1 -> x0, blocking collectives: 24.4 us -> none  [local(): lax.all_to_all(attended, 'tensor', split_axis=1, concat_axis=0, tiled=True)]
    reduce_scatter x1 -> x2, waiting for transfers between devices: 66 us -> 53.7 us  [the longest x1 39.3 us: local(): lax.psum_scatter(partial, 'tensor', scatter_dimension=0, tiled=True)]
    all_to_all x1 -> x2, starting transfers between devices: 6.73 us -> 14.2 us  [the longest x1 8.57 us: local(): lax.all_to_all(attended, 'tensor', split_axis=1, concat_axis=0, tiled=True)]
    unnamed x43 -> x31, local copies, waits for them, and re-layouts: 5.36 us -> 11.5 us
  transfers between devices with their start and end apart: 6 -> 8, of which waited for: 4 -> 7; matrix products, arithmetic and copies ran while one was open for 3% -> 4% of each run, Pallas kernels for 0% -> 0%
where the time goes in v2:
time: 393 us; the launch traced here: 392 us
  waiting for transfers between devices  227 us (58%)
  blocking collectives  50.9 us (13%)
  matrix products  37.4 us (10%)
  local copies, waits for them, and re-layouts  29.4 us (7%)
  starting transfers between devices  21.4 us (5%)
  between operations  13.4 us (3%)
  other arithmetic  12 us (3%)
    all_to_all x1, waiting for transfers between devices, local(): lax.all_to_all(down_pack, RT, split_axis=1, concat_axis=0, tiled=True)  57.4 us
    all_gather x1, waiting for transfers between devices, local(): collected_rows = lax.all_gather(picked, RT, axis=0, tiled=True)  54.9 us
    all_gather x1, waiting for transfers between devices, local(): gathered = lax.all_gather(hidden_ext, RT, axis=0, tiled=True)  40.4 us
    reduce_scatter x1, waiting for transfers between devices, local(): lax.psum_scatter(partial, 'tensor', scatter_dimension=0, tiled=True)  39.3 us
    all_gather x1, blocking collectives, local(): lax.all_gather(mixed_in.reshape(-1, 128), 'dp', axis=0, tiled=True)  26.3 us
    all_to_all x1, blocking collectives, local(): lax.all_to_all(expert_out, RT, split_axis=0, concat_axis=0, tiled=True)  24.5 us
    reduce_scatter x1, waiting for transfers between devices, local(): partial = lax.psum_scatter(partial, 'role', scatter_dimension=0, tiled=True)  14.4 us
    all_to_all x1, waiting for transfers between devices, local(): lax.all_to_all(by_group, 'dp', split_axis=0, concat_axis=0, tiled=True)  12.1 us
  transfers between devices with their start and end apart: 8, of which 7 were waited for; matrix products, arithmetic and copies ran while one was open for 4% of the time, Pallas kernels for 0%

profile of v2, /device:TPU:32, one launch (start us, length us, event | category | flops | bytes accessed | tf_op | source)
XLA Modules:
  0.0 392.1 jit_solution(4782587846072727202)
XLA Ops:
  6.5 0.9 iota_compare_fusion.4
  7.4 0.7 reshape.194
  8.2 3.9 fusion.9
  12.1 0.4 fusion.66
  12.5 2.5 fusion.2
  15.1 0.6 fusion.14
  15.7 0.1 copy-done.7
  15.8 1.6 fusion.19
  17.4 1.1 copy.61
  18.5 8.6 %all-to-all-start.1 = ((bf16[8,64,512]{2,0,1:T(8,128)(2,1)}), bf16[8,64,512]{2,0,1:T(8,128)(2,1)S(1)}, u32[]{:S(2)}, u32[]{:S(2)}) async-start(bf16[8,64,512]{2,0,1:T(8,128)(2,1)} %copy.61), calls=%async_computation.1 | async-start | bytes 1048576 | tf_op jit(solution)/shard_map/all_to_all | solution.py:105
  27.1 3.9 copy.58
  31.0 0.1 broadcast_in_dim.25
  31.1 3.2 pad_maximum_fusion
  34.3 8.8 %all-to-all-done.1 = bf16[8,64,512]{2,0,1:T(8,128)(2,1)S(1)} async-done(((bf16[8,64,512]{2,0,1:T(8,128)(2,1)}), bf16[8,64,512]{2,0,1:T(8,128)(2,1)S(1)}, u32[]{:S(2)}, u32[]{:S(2)}) %all-to-all-start.1) | async-done | bytes 524320 | tf_op jit(solution)/shard_map/all_to_all | solution.py:105
  43.1 5.7 %all-to-all-start = ((bf16[128,16,640]{0,2,1:T(8,128)(2,1)}), bf16[128,16,640]{0,2,1:T(8,128)(2,1)}, u32[]{:S(2)}, u32[]{:S(2)}) async-start(bf16[128,16,640]{0,2,1:T(8,128)(2,1)} %pad_maximum_fusion), calls=%async_computation | async-start | bytes 5242880 | tf_op jit(solution)/shard_map/all_to_all | solution.py:67
  48.8 0.0 all-gather.4.cloned.1.call-start
  48.8 1.5 fusion.27
  50.4 0.7 copy.92
  51.0 0.0 all-gather.4.cloned.1.call-update
  51.1 0.0 reduce-scatter.5.cloned.1.call-start
  51.1 57.4 %all-to-all-done = bf16[128,16,640]{0,2,1:T(8,128)(2,1)} async-done(((bf16[128,16,640]{0,2,1:T(8,128)(2,1)}), bf16[128,16,640]{0,2,1:T(8,128)(2,1)}, u32[]{:S(2)}, u32[]{:S(2)}) %all-to-all-start) | async-done | bytes 2621472 | tf_op jit(solution)/shard_map/all_to_all | solution.py:67
  108.6 4.4 %copy.59 = bf16[16,128,1,640]{3,1,0,2:T(8,128)(2,1)} copy(bf16[16,128,1,640]{1,3,0,2:T(8,128)(2,1)} %bitcast.5) | data formatting | bytes 5242880 | tf_op jit(solution)/shard_map/all_to_all | solution.py:67
  113.0 4.3 %fusion.67 = f32[1024,448]{0,1:T(8,128)} fusion(bf16[1024,1024]{1,0:T(8,128)(2,1)} %all-gather.4.cloned.1.call-done, bf16[1024,448]{0,1:T(8,128)(2,1)} %param.23), kind=kOutput, calls=%fused_computation.89 | convolution fusion | flops 939524096 | bytes 4849664 | tf_op jit(solution)/shard_map/dot_general | solution.py:114
  117.3 0.0 reduce-scatter.5.cloned.1.call-update
  117.3 0.0 reduce-scatter.7.cloned.1.call-start
  117.3 14.4 %reduce-scatter.5.cloned.1.call-done = f32[512,448]{0,1:T(8,128)} async-done(((f32[1024,448]{0,1:T(8,128)}), f32[512,448]{0,1:T(8,128)}) %reduce-scatter.5.cloned.1.call-update) | async-done | bytes 917520 | tf_op jit(solution)/shard_map/reduce_scatter | solution.py:115
  131.7 2.5 copy.75
  134.2 0.0 reduce-scatter.7.cloned.1.call-update
  134.2 0.0 all-gather.6.cloned.1.call-start
  134.3 0.2 reduce_window_sum.11
  134.6 0.1 reshape.191
  134.7 0.1 fusion.43
  134.7 39.3 %reduce-scatter.7.cloned.1.call-done = f32[64,448]{1,0:T(8,128)} async-done(((f32[512,448]{1,0:T(8,128)}), f32[64,448]{1,0:T(8,128)}) %reduce-scatter.7.cloned.1.call-update) | async-done | bytes 114704 | tf_op jit(solution)/shard_map/reduce_scatter | solution.py:116
  174.0 0.9 add_convert_fusion
  175.0 0.1 reshape.184
  175.1 26.3 %all_gather.13 = bf16[3584,128]{1,0:T(8,128)(2,1)} all-gather(bf16[224,128]{1,0:T(8,128)(2,1)S(1)} %reshape.184), channel_id=1, replica_groups=mesh['role'=2,'dp'=16,'tensor'=8] {'dp'}, dimensions={0}, use_global_device_ids=true | all-gather | bytes 974848 | tf_op jit(solution)/shard_map/all_gather | solution.py:121
  201.4 2.9 reshape.190
  204.3 2.1 multiply_reduce_fusion
  206.4 0.1 copy-done.1
  206.5 2.3 fusion.31
  208.9 2.9 convert_element_type.116
  211.8 2.3 convolution_convert_fusion
  214.1 0.0 all-gather.6.cloned.1.call-update
  214.1 0.2 all-gather.8.cloned.1.call-start
  214.3 0.1 select_reduce_fusion.1
  214.5 54.9 %all-gather.6.cloned.1.call-done = bf16[640,7168]{1,0:T(8,128)(2,1)} async-done(((bf16[40,7168]{1,0:T(8,128)(2,1)}), bf16[640,7168]{1,0:T(8,128)(2,1)}) %all-gather.6.cloned.1.call-update) | async-done | bytes 9175056 | tf_op jit(solution)/shard_map/all_gather | solution.py:128
  269.4 6.8 %fusion.12 = f32[640,128]{1,0:T(8,128)S(1)} fusion(bf16[640,7168]{1,0:T(8,128)(2,1)} %all-gather.6.cloned.1.call-done, bf16[1,7168,128]{2,1,0:T(8,128)(2,1)} %param.29), kind=kOutput, calls=%fused_computation.18 | convolution fusion | flops 1174405120 | bytes 11337728 | tf_op jit(solution)/shard_map/dot_general | solution.py:129
  276.2 0.4 copy-done.13
  276.7 2.5 fusion.23
  279.2 0.7 fusion.47
  279.9 0.0 all-gather.8.cloned.1.call-update
  279.9 40.4 %all-gather.8.cloned.1.call-done = bf16[10368,128]{1,0:T(8,128)(2,1)} async-done(((bf16[648,128]{1,0:T(8,128)(2,1)}), bf16[10368,128]{1,0:T(8,128)(2,1)}) %all-gather.8.cloned.1.call-update) | async-done | bytes 2654224 | tf_op jit(solution)/shard_map/all_gather | solution.py:137
  320.3 3.5 slice.41
  323.8 4.4 %copy.78 = bf16[16,640,128]{1,2,0:T(8,128)(2,1)} copy(bf16[16,640,128]{2,1,0:T(8,128)(2,1)} %slice.41) | data formatting | bytes 5242880
  328.2 5.2 %fusion.5 = f32[640,448]{0,1:T(8,128)} fusion(bf16[640,2048]{0,1:T(8,128)(2,1)} %bitcast.106, bf16[2048,640]{1,0:T(8,128)(2,1)} %bitcast.104), kind=kOutput, calls=%fused_computation.7 | convolution fusion | flops 1174405120 | bytes 5865472 | tf_op jit(solution)/shard_map/dot_general | solution.py:144
  333.4 2.4 fusion.32
  335.8 0.8 fusion.55
  336.6 0.1 reshape.192
  336.7 2.9 fusion.18
  339.6 1.3 copy.69
  340.9 24.5 %all_to_all.46 = bf16[16,40,448]{2,1,0:T(8,128)(2,1)} all-to-all(bf16[16,40,448]{2,1,0:T(8,128)(2,1)S(1)} %bitcast.108), channel_id=1, replica_groups=mesh['role'=2,'dp'=16,'tensor'=8] {'role','tensor'}, dimensions={0} | all-to-all | bytes 1146880 | tf_op jit(solution)/shard_map/all_to_all | solution.py:154
  365.4 6.8 %all-to-all-start.3 = ((bf16[16,40,448]{2,1,0:T(8,128)(2,1)}), bf16[16,40,448]{2,1,0:T(8,128)(2,1)S(1)}, u32[]{:S(2)}, u32[]{:S(2)}) async-start(bf16[16,40,448]{2,1,0:T(8,128)(2,1)} %all_to_all.46), calls=%async_computation.4 | async-start | bytes 1310720 | tf_op jit(solution)/shard_map/all_to_all | solution.py:155
  372.3 12.1 %all-to-all-done.3 = bf16[16,40,448]{2,1,0:T(8,128)(2,1)S(1)} async-done(((bf16[16,40,448]{2,1,0:T(8,128)(2,1)}), bf16[16,40,448]{2,1,0:T(8,128)(2,1)S(1)}, u32[]{:S(2)}, u32[]{:S(2)}) %all-to-all-start.3) | async-done | bytes 573472 | tf_op jit(solution)/shard_map/all_to_all | solution.py:155
  384.4 1.1 fusion.28
  (38 shorter events, 0.2 us)
Async XLA Ops:
  6.5 330.1 %copy-start = (bf16[3,1,64,7168]{3,2,1,0:T(8,128)(2,1)S(1)}, bf16[3,1,64,7168]{3,2,1,0:T(8,128)(2,1)}, u32[]{:S(2)}) copy-start(bf16[3,1,64,7168]{3,2,1,0:T(8,128)(2,1)} %param.33) | copy-start | bytes 8257540
  8.1 3.9 %copy-start.4 = (bf16[8,64,576]{2,1,0:T(8,128)(2,1)S(1)}, bf16[8,64,576]{2,1,0:T(8,128)(2,1)}, u32[]{:S(2)}) copy-start(bf16[8,64,576]{2,1,0:T(8,128)(2,1)} %param.18) | copy-start | bytes 1769476
  8.1 4.4 %copy-start.2 = (bf16[4,1024,576]{1,2,0:T(8,128)(2,1)S(1)}, bf16[4,1024,576]{1,2,0:T(8,128)(2,1)}, u32[]{:S(2)}) copy-start(bf16[4,1024,576]{1,2,0:T(8,128)(2,1)} %param.19) | copy-start | bytes 14155780
  15.1 0.7 copy-start.7
  18.5 24.6 %all-to-all-start.1 = ((bf16[8,64,512]{2,0,1:T(8,128)(2,1)}), bf16[8,64,512]{2,0,1:T(8,128)(2,1)S(1)}, u32[]{:S(2)}, u32[]{:S(2)}) async-start(bf16[8,64,512]{2,0,1:T(8,128)(2,1)} %copy.61), calls=%async_computation.1 | async-start | bytes 1048576 | tf_op jit(solution)/shard_map/all_to_all | solution.py:105
  27.1 3.9 copy-start.6
  43.1 65.4 %all-to-all-start = ((bf16[128,16,640]{0,2,1:T(8,128)(2,1)}), bf16[128,16,640]{0,2,1:T(8,128)(2,1)}, u32[]{:S(2)}, u32[]{:S(2)}) async-start(bf16[128,16,640]{0,2,1:T(8,128)(2,1)} %pad_maximum_fusion), calls=%async_computation | async-start | bytes 5242880 | tf_op jit(solution)/shard_map/all_to_all | solution.py:67
  48.8 64.2 %all-gather.4.cloned.1.call-start = ((), (), s32[]{:S(2)}) async-start(), calls=%async_computation.6 | async-start | bytes 2228224 | tf_op jit(solution)/shard_map/all_gather | solution.py:112
  51.1 80.6 %reduce-scatter.5.cloned.1.call-start = ((), (), s32[]{:S(2)}) async-start(), calls=%async_computation.7 | async-start | bytes 2752512 | tf_op jit(solution)/shard_map/reduce_scatter | solution.py:115
  117.2 17.0 %copy-start.8 = (s32[64,8]{0,1:T(8,128)S(1)}, s32[64,8]{0,1:T(8,128)}, u32[]{:S(2)}) copy-start(s32[64,8]{0,1:T(8,128)} %param.26) | copy-start | bytes 6148
  117.2 17.3 %copy-start.9 = (bf16[7168]{0:T(1024)(128)(2,1)S(1)}, bf16[7168]{0:T(1024)(128)(2,1)}, u32[]{:S(2)}) copy-start(bf16[7168]{0:T(1024)(128)(2,1)} %param.25) | copy-start | bytes 43012
  117.2 56.8 %copy-start.5 = (bf16[64,448]{1,0:T(8,128)(2,1)S(1)}, bf16[64,448]{1,0:T(8,128)(2,1)}, u32[]{:S(2)}) copy-start(bf16[64,448]{1,0:T(8,128)(2,1)} %param.24) | copy-start | bytes 172036
  117.3 56.8 %reduce-scatter.7.cloned.1.call-start = ((), (), s32[]{:S(2)}) async-start(), calls=%async_computation.10 | async-start | bytes 1179648 | tf_op jit(solution)/shard_map/reduce_scatter | solution.py:116
  134.2 135.2 %all-gather.6.cloned.1.call-start = ((), (), s32[]{:S(2)}) async-start(), calls=%async_computation.8 | async-start | bytes 9748480 | tf_op jit(solution)/shard_map/all_gather | solution.py:128
  204.3 2.2 copy-start.1
  208.9 5.5 %copy-start.11 = (s32[64]{0:T(128)S(1)}, s32[64]{0:T(128)}, u32[]{:S(2)}) copy-start(s32[64]{0:T(128)} %param.28) | copy-start | bytes 772
  214.1 106.2 %all-gather.8.cloned.1.call-start = ((), (), s32[]{:S(2)}) async-start(), calls=%async_computation.9 | async-start | bytes 2820096 | tf_op jit(solution)/shard_map/all_gather | solution.py:137
  269.4 6.8 %copy-start.12 = (bf16[640,7168]{1,0:T(8,128)(2,1)S(1)}, bf16[640,7168]{1,0:T(8,128)(2,1)}, u32[]{:S(2)}) copy-start(bf16[640,7168]{1,0:T(8,128)(2,1)} %all-gather.6.cloned.1.call-done) | copy-start | bytes 27525124
  269.4 7.2 %copy-start.13 = (bf16[1,7168,128]{2,1,0:T(8,128)(2,1)S(1)}, bf16[1,7168,128]{2,1,0:T(8,128)(2,1)}, u32[]{:S(2)}) copy-start(bf16[1,7168,128]{2,1,0:T(8,128)(2,1)} %param.30) | copy-start | bytes 5505028
  328.2 5.2 %copy-start.3 = (bf16[16,640,128]{1,2,0:T(8,128)(2,1)S(1)}, bf16[16,640,128]{1,2,0:T(8,128)(2,1)}, u32[]{:S(2)}) copy-start(bf16[16,640,128]{1,2,0:T(8,128)(2,1)} %copy.78) | copy-start | bytes 7864324
  339.6 32.7 %copy-start.10 = (f32[64,8]{0,1:T(8,128)S(1)}, f32[64,8]{0,1:T(8,128)}, u32[]{:S(2)}) copy-start(f32[64,8]{0,1:T(8,128)} %param.27) | copy-start | bytes 6148
  365.4 19.0 %all-to-all-start.3 = ((bf16[16,40,448]{2,1,0:T(8,128)(2,1)}), bf16[16,40,448]{2,1,0:T(8,128)(2,1)S(1)}, u32[]{:S(2)}, u32[]{:S(2)}) async-start(bf16[16,40,448]{2,1,0:T(8,128)(2,1)} %all_to_all.46), calls=%async_computation.4 | async-start | bytes 1310720 | tf_op jit(solution)/shard_map/all_to_all | solution.py:155
Sparse Core Ops, SparseCore 0:
  52.0 51.1 all-gather.3
  117.4 14.2 reduce-scatter.4
  134.3 39.6 reduce-scatter.6
  214.2 55.1 all-gather.5
  280.0 40.2 all-gather.7

commit v3 on v2

--- a/solution.py
+++ b/solution.py
@@ -64,6 +64,13 @@
     left_local = jnp.transpose(left_local, (1, 0, 2)).reshape(hidden_slice, 1, tenants * rank)
     left_local = jnp.broadcast_to(left_local, (hidden_slice, n_slices, tenants * rank))
     down_pack = jnp.concatenate([down_local, left_local], axis=2)
+    pack_width = down_pack.shape[2]
+    slot_token = jnp.sum(mine.astype(jnp.int32) * jnp.arange(group_rows, dtype=jnp.int32)[None, :], axis=1)
+    slot_used = jnp.sum(mine.astype(jnp.int32), axis=1)
+    info = jnp.concatenate([slot_token, slot_used, mine_owner]).astype(jnp.bfloat16)
+    info_rows = jnp.zeros((8, pack_width), jnp.bfloat16).at[0, : info.shape[0]].set(info)
+    info_rows = jnp.broadcast_to(info_rows[:, None, :], (8, n_slices, pack_width))
+    down_pack = jnp.concatenate([down_pack, info_rows], axis=0)
     down_pack = lax.all_to_all(down_pack, RT, split_axis=1, concat_axis=0, tiled=True)
     right_w = lax.dynamic_slice_in_dim(factor_right[:, 0], slice_idx * col_width, col_width, 2)
 
@@ -118,27 +125,29 @@
         (residual.astype(jnp.float32) + attention).astype(jnp.bfloat16)
     )
 
-    full_rows = lax.all_gather(mixed_in.reshape(-1, 128), "dp", axis=0, tiled=True)
-    full_rows = full_rows.reshape(-1, group_rows, mixed_in.shape[1])
-    full_rows = jnp.transpose(full_rows, (1, 0, 2)).reshape(group_rows, model_width)
-    normed = rms_rows(full_rows, norm_gain)
-    picked = jnp.dot(
-        mine.astype(jnp.bfloat16), normed, preferred_element_type=jnp.float32
-    ).astype(jnp.bfloat16)
-    collected_rows = lax.all_gather(picked, RT, axis=0, tiled=True)
+    down_pack = down_pack.reshape(n_slices, hidden_slice + 8, pack_width)
+    info = down_pack[:, hidden_slice, : 3 * capacity].astype(jnp.int32)
+    slot_token, slot_used, owners = info[:, :capacity], info[:, capacity : 2 * capacity], info[:, 2 * capacity :]
+    owners = owners.reshape(n_slices * capacity)
+    n_cols = lax.axis_size("dp")
+    everything = lax.all_gather(mixed_in, ("role", "tensor", "dp"), axis=0, tiled=True)
+    everything = everything.reshape(n_slices, n_cols, group_rows, mixed_in.shape[1])
+    one_hot = (slot_token[:, :, None] == jnp.arange(group_rows, dtype=jnp.int32)[None, None, :]) & (
+        slot_used[:, :, None] > 0
+    )
+    picked = jnp.einsum(
+        "ncg,ndgk->ncdk", one_hot.astype(jnp.bfloat16), everything, preferred_element_type=jnp.float32
+    )
+    picked = picked.reshape(n_slices * capacity, model_width)
+    scale = lax.rsqrt(jnp.mean(picked * picked, axis=-1, keepdims=True) + NORM_EPS)
+    collected_rows = (picked * scale * norm_gain.astype(jnp.float32)).astype(jnp.bfloat16)
     gate_scores = jnp.dot(collected_rows, expert_gate_weight[0], preferred_element_type=jnp.float32)
     upper_bound = jnp.dot(collected_rows, expert_up_weight[0], preferred_element_type=jnp.float32)
     hidden = (jax.nn.silu(gate_scores) * upper_bound).astype(jnp.bfloat16)
 
-    lanes = hidden.shape[1]
-    owner_block = jnp.zeros((8, lanes), jnp.bfloat16)
-    owner_block = owner_block.at[0, :capacity].set(mine_owner.astype(jnp.bfloat16))
-    hidden_ext = jnp.concatenate([hidden, owner_block], axis=0)
-    gathered = lax.all_gather(hidden_ext, RT, axis=0, tiled=True)
-    gathered = gathered.reshape(n_slices, hidden.shape[0] + 8, lanes)
-    owners = gathered[:, hidden.shape[0], :capacity].astype(jnp.int32).reshape(n_slices * capacity)
-    hidden_all = jnp.transpose(gathered[:, : hidden.shape[0]], (1, 0, 2)).reshape(hidden.shape[0], -1)
-    down_pack = down_pack.reshape(n_slices * hidden_slice, col_width + tenants * rank)
+    gathered = lax.all_gather(hidden, RT, axis=0, tiled=False)
+    hidden_all = jnp.transpose(gathered, (1, 0, 2)).reshape(hidden.shape[0], -1)
+    down_pack = down_pack[:, :hidden_slice].reshape(n_slices * hidden_slice, pack_width)
     down_w = down_pack[:, :col_width]
     left_w = down_pack[:, col_width:].reshape(n_slices * hidden_slice, tenants, rank)
     base_output = jnp.dot(hidden_all, down_w, preferred_element_type=jnp.float32)

time: 393 us -> 473 us (1.20)
  waiting for transfers between devices: 227 us -> 286 us
  local copies, waits for them, and re-layouts: 29.4 us -> 58.4 us
  blocking collectives: 50.9 us -> 24.5 us
  other arithmetic: 12 us -> 21.3 us
  matrix products: 37.4 us -> 44.8 us
    all_gather x2, waiting for transfers between devices: 95.3 us -> 158 us  [the longest x1 125 us: local(): lax.all_gather(mixed_in, ('role', 'tensor', 'dp'), axis=0, tiled=True)]
    all_gather x1, waiting for transfers between devices: 0.01 us -> 52.1 us  [local(): all_values = lax.all_gather(head_values, 'dp', axis=0, tiled=True)]
    all_to_all x1, waiting for transfers between devices: 57.4 us -> 8.75 us  [local(): lax.all_to_all(down_pack, RT, split_axis=1, concat_axis=0, tiled=True)]
    all_gather x1 -> x0, blocking collectives: 26.3 us -> none  [local(): lax.all_gather(mixed_in.reshape(-1, 128), 'dp', axis=0, tiled=True)]
    convert_element_type x3 -> x2, local copies, waits for them, and re-layouts: 5.86 us -> 30.8 us  [local(): (picked * scale * norm_gain.astype(jnp.float32)).astype(jnp.bfloat16)]
    convert_element_type x3 -> x2, other arithmetic: 3.14 us -> 14.2 us  [the longest x1 13.5 us: local(): (picked * scale * norm_gain.astype(jnp.float32)).astype(jnp.bfloat16)]
    dot_general x1, matrix products: 2.28 us -> 11.9 us  [local(): jnp.einsum('ncg,ndgk->ncdk', one_hot.astype(jnp.bfloat16), everything, pr...]
    all_to_all x1, waiting for transfers between devices: 8.79 us -> 0.18 us  [local(): lax.all_to_all(attended, 'tensor', split_axis=1, concat_axis=0, tiled=True)]
  transfers between devices with their start and end apart: 8 -> 8, of which waited for: 7 -> 8; matrix products, arithmetic and copies ran while one was open for 4% -> 5% of each run, Pallas kernels for 0% -> 0%
where the time goes in v3:
time: 473 us; the launch traced here: 471 us
  waiting for transfers between devices  286 us (60%)
  local copies, waits for them, and re-layouts  58.4 us (12%)
  matrix products  44.8 us (9%)
  blocking collectives  24.5 us (5%)
  starting transfers between devices  22.9 us (5%)
  other arithmetic  21.3 us (5%)
  between operations  13.4 us (3%)
    all_gather x1, waiting for transfers between devices, local(): lax.all_gather(mixed_in, ('role', 'tensor', 'dp'), axis=0, tiled=True)  125 us
    all_gather x1, waiting for transfers between devices, local(): all_values = lax.all_gather(head_values, 'dp', axis=0, tiled=True)  52.1 us
    reduce_scatter x1, waiting for transfers between devices, local(): lax.psum_scatter(partial, 'tensor', scatter_dimension=0, tiled=True)  39.8 us
    all_gather x1, waiting for transfers between devices, local(): gathered = lax.all_gather(hidden, RT, axis=0, tiled=False)  33.6 us
    convert_element_type x2, local copies, waits for them, and re-layouts, local(): (picked * scale * norm_gain.astype(jnp.float32)).astype(jnp.bfloat16)  30.8 us
    all_to_all x1, blocking collectives, local(): lax.all_to_all(expert_out, RT, split_axis=0, concat_axis=0, tiled=True)  24.5 us
    reduce_scatter x1, waiting for transfers between devices, local(): partial = lax.psum_scatter(partial, 'role', scatter_dimension=0, tiled=True)  14.5 us
    convert_element_type x1, other arithmetic, local(): (picked * scale * norm_gain.astype(jnp.float32)).astype(jnp.bfloat16)  13.5 us
  transfers between devices with their start and end apart: 8, of which 8 were waited for; matrix products, arithmetic and copies ran while one was open for 5% of the time, Pallas kernels for 0%

profile of v3, /device:TPU:32, one launch (start us, length us, event | category | flops | bytes accessed | tf_op | source)
XLA Modules:
  0.0 471.5 jit_solution(3004877601197552970)
XLA Ops:
  6.5 0.9 reshape.238
  7.4 0.7 reshape.225
  8.1 0.7 iota_compare_fusion.4
  8.9 1.7 fusion.64
  10.5 3.8 fusion.7
  14.4 0.6 fusion.12
  15.0 1.7 fusion.2
  16.8 0.4 fusion.17
  17.1 1.1 copy.65
  18.3 8.7 %all-to-all-start.1 = ((bf16[8,64,512]{2,0,1:T(8,128)(2,1)}), bf16[8,64,512]{2,0,1:T(8,128)(2,1)S(1)}, u32[]{:S(2)}, u32[]{:S(2)}) async-start(bf16[8,64,512]{2,0,1:T(8,128)(2,1)} %copy.65), calls=%async_computation.1 | async-start | bytes 1048576 | tf_op jit(solution)/shard_map/all_to_all | solution.py:112
  27.0 0.2 reduce_window_sum.11
  27.3 0.1 fusion.39
  27.3 0.2 select_reduce_fusion.2
  27.5 0.1 pad_maximum_fusion.1
  27.6 0.1 copy.83
  27.7 3.9 copy.61
  31.7 0.5 broadcast_in_dim.28
  32.2 0.9 copy-done.2
  33.1 3.5 pad_maximum_fusion
  36.6 6.2 %copy.63 = bf16[136,16,640]{2,0,1:T(8,128)(2,1)} copy(bf16[136,16,640]{0,2,1:T(8,128)(2,1)} %pad_maximum_fusion) | data formatting | bytes 5570560 | tf_op jit(solution)/shard_map/concatenate | solution.py:73
  42.9 0.2 all-to-all-done.1
  43.0 7.0 %all-to-all-start = ((bf16[136,16,640]{2,0,1:T(8,128)(2,1)}), bf16[136,16,640]{2,0,1:T(8,128)(2,1)}, u32[]{:S(2)}, u32[]{:S(2)}) async-start(bf16[136,16,640]{2,0,1:T(8,128)(2,1)} %copy.63), calls=%async_computation | async-start | bytes 5570560 | tf_op jit(solution)/shard_map/all_to_all | solution.py:74
  50.1 0.0 all-gather.5.cloned.1.call-start
  50.1 1.5 fusion.25
  51.7 0.7 copy.90
  52.4 0.0 all-gather.5.cloned.1.call-update
  52.4 0.0 reduce-scatter.5.cloned.1.call-start
  52.4 52.1 %all-gather.5.cloned.1.call-done = bf16[1024,1024]{1,0:T(8,128)(2,1)} async-done(((bf16[64,1024]{1,0:T(8,128)(2,1)}), bf16[1024,1024]{1,0:T(8,128)(2,1)}) %all-gather.5.cloned.1.call-update) | async-done | bytes 2097168 | tf_op jit(solution)/shard_map/all_gather | solution.py:119
  104.5 8.7 %all-to-all-done = bf16[136,16,640]{2,0,1:T(8,128)(2,1)} async-done(((bf16[136,16,640]{2,0,1:T(8,128)(2,1)}), bf16[136,16,640]{2,0,1:T(8,128)(2,1)}, u32[]{:S(2)}, u32[]{:S(2)}) %all-to-all-start) | async-done | bytes 2785312 | tf_op jit(solution)/shard_map/all_to_all | solution.py:74
  113.2 4.2 fusion.65
  117.4 0.0 reduce-scatter.5.cloned.1.call-update
  117.5 0.0 reduce-scatter.7.cloned.1.call-start
  117.5 14.5 %reduce-scatter.5.cloned.1.call-done = f32[512,448]{0,1:T(8,128)} async-done(((f32[1024,448]{0,1:T(8,128)}), f32[512,448]{0,1:T(8,128)}) %reduce-scatter.5.cloned.1.call-update) | async-done | bytes 917520 | tf_op jit(solution)/shard_map/reduce_scatter | solution.py:122
  132.0 2.5 copy.80
  134.5 0.0 reduce-scatter.7.cloned.1.call-update
  134.5 0.0 all-gather.7.cloned.1.call-start
  134.6 39.8 %reduce-scatter.7.cloned.1.call-done = f32[64,448]{1,0:T(8,128)} async-done(((f32[512,448]{1,0:T(8,128)}), f32[64,448]{1,0:T(8,128)}) %reduce-scatter.7.cloned.1.call-update) | async-done | bytes 114704 | tf_op jit(solution)/shard_map/reduce_scatter | solution.py:123
  174.4 1.5 add_convert_fusion
  175.9 0.0 all-gather.7.cloned.1.call-update
  175.9 0.2 all-gather.9.cloned.1.call-start
  176.2 0.1 reshape.235
  176.2 0.8 slice_convert_fusion
  177.0 0.1 slice_compare_fusion
  177.1 0.1 fusion.63
  177.2 124.9 %all-gather.7.cloned.1.call-done = bf16[16384,448]{1,0:T(8,128)(2,1)} async-done(((bf16[64,448]{1,0:T(8,128)(2,1)}), bf16[16384,448]{1,0:T(8,128)(2,1)}) %all-gather.7.cloned.1.call-update) | async-done | bytes 14680080 | tf_op jit(solution)/shard_map/all_gather | solution.py:133
  302.0 11.9 %multiply_reduce_fusion = (f32[16,40]{1,0:T(8,128)S(1)}, f32[16,40,16,448]{3,1,2,0:T(8,128)}) fusion(bf16[16,16,64,448]{3,2,1,0:T(8,128)(2,1)} %bitcast.118, s32[16,40]{1,0:T(8,128)S(1)} %get-tuple-element.25, pred[16,40]{1,0:T(8,128)(4,1)S(1)} %slice_compare_fusion), kind=kOutput, calls=%fused_computation.1 | convolution fusion | flops 596458880 | bytes 33035904 | tf_op jit(solution)/shard_map/ncg,ndgk->ncdk/dot_general | solution.py:138
  314.0 13.5 %multiply_convert_fusion = bf16[16,40,16,448]{3,1,2,0:T(8,128)(2,1)} fusion(f32[16,40,16,448]{3,1,2,0:T(8,128)} %get-tuple-element.33, f32[16,448]{1,0:T(8,128)S(1)} %reshape.235, f32[16,40]{1,0:T(8,128)S(1)} %add_rsqrt_fusion), kind=kLoop, calls=%fused_computation | loop fusion | flops 13762560 | bytes 27556352 | tf_op jit(solution)/shard_map/convert_element_type | solution.py:143
  327.5 12.4 %copy.69 = bf16[16,40,16,448]{3,2,1,0:T(8,128)(2,1)} copy(bf16[16,40,16,448]{3,1,2,0:T(8,128)(2,1)} %multiply_convert_fusion) | data formatting | bytes 18350080 | tf_op jit(solution)/shard_map/convert_element_type | solution.py:143
  339.9 18.4 %convert_element_type.97 = bf16[640,7168]{1,0:T(8,128)(2,1)} reshape(bf16[16,40,16,448]{3,2,1,0:T(8,128)(2,1)} %copy.69) | data formatting | bytes 18350080 | tf_op jit(solution)/shard_map/convert_element_type | solution.py:143
  358.3 6.8 %fusion.10 = f32[640,128]{1,0:T(8,128)S(1)} fusion(bf16[640,7168]{1,0:T(8,128)(2,1)} %convert_element_type.97, bf16[1,7168,128]{2,1,0:T(8,128)(2,1)} %param.29), kind=kOutput, calls=%fused_computation.15 | convolution fusion | flops 1174405120 | bytes 11337728 | tf_op jit(solution)/shard_map/dot_general | solution.py:144
  365.0 0.4 copy-done.11
  365.5 3.2 fusion.21
  368.7 3.6 slice.56
  372.3 0.1 eq.83
  372.4 33.6 %all-gather.9.cloned.1.call-done = bf16[10240,128]{1,0:T(8,128)(2,1)} async-done(((bf16[640,128]{1,0:T(8,128)(2,1)}), bf16[10240,128]{1,0:T(8,128)(2,1)}) %all-gather.9.cloned.1.call-update) | async-done | bytes 2621456 | tf_op jit(solution)/shard_map/all_gather | solution.py:148
  406.0 4.4 copy.70
  410.4 3.4 fusion.29
  413.8 3.4 fusion.5
  417.3 1.7 fusion.16
  419.0 1.3 copy.73
  420.3 24.5 %all_to_all.46 = bf16[16,40,448]{2,1,0:T(8,128)(2,1)} all-to-all(bf16[16,40,448]{2,1,0:T(8,128)(2,1)S(1)} %bitcast.127), channel_id=1, replica_groups=mesh['role'=2,'dp'=16,'tensor'=8] {'role','tensor'}, dimensions={0} | all-to-all | bytes 1146880 | tf_op jit(solution)/shard_map/all_to_all | solution.py:163
  444.8 6.8 %all-to-all-start.3 = ((bf16[16,40,448]{2,1,0:T(8,128)(2,1)}), bf16[16,40,448]{2,1,0:T(8,128)(2,1)S(1)}, u32[]{:S(2)}, u32[]{:S(2)}) async-start(bf16[16,40,448]{2,1,0:T(8,128)(2,1)} %all_to_all.46), calls=%async_computation.4 | async-start | bytes 1310720 | tf_op jit(solution)/shard_map/all_to_all | solution.py:164
  451.7 12.1 %all-to-all-done.3 = bf16[16,40,448]{2,1,0:T(8,128)(2,1)S(1)} async-done(((bf16[16,40,448]{2,1,0:T(8,128)(2,1)}), bf16[16,40,448]{2,1,0:T(8,128)(2,1)S(1)}, u32[]{:S(2)}, u32[]{:S(2)}) %all-to-all-start.3) | async-done | bytes 573472 | tf_op jit(solution)/shard_map/all_to_all | solution.py:164
  463.8 1.1 fusion.26
  (42 shorter events, 0.3 us)
Async XLA Ops:
  6.5 410.7 %copy-start = (bf16[3,1,64,7168]{3,2,1,0:T(8,128)(2,1)S(1)}, bf16[3,1,64,7168]{3,2,1,0:T(8,128)(2,1)}, u32[]{:S(2)}) copy-start(bf16[3,1,64,7168]{3,2,1,0:T(8,128)(2,1)} %param.33) | copy-start | bytes 8257540
  8.9 6.1 %slice-start = ((s8[4718592]{0:T(1024)(128)(4,1)}), s8[4194304]{0:T(1024)(128)(4,1)S(1)}, s32[]{:S(2)}) async-start(s8[4718592]{0:T(1024)(128)(4,1)} %bitcast.120), calls=%async_computation.11 | async-start | bytes 8388608
  10.5 4.4 slice-start.1
  16.8 10.2 %copy-start.7 = (s32[64,8]{0,1:T(8,128)S(1)}, s32[64,8]{0,1:T(8,128)}, u32[]{:S(2)}) copy-start(s32[64,8]{0,1:T(8,128)} %param.26) | copy-start | bytes 6148
  16.8 10.6 %copy-start.10 = (s32[64]{0:T(128)S(1)}, s32[64]{0:T(128)}, u32[]{:S(2)}) copy-start(s32[64]{0:T(128)} %param.28) | copy-start | bytes 772
  18.3 13.4 %copy-start.6 = (bf16[3,1,128,64]{2,3,1,0:T(8,128)(2,1)S(1)}, bf16[3,1,128,64]{2,3,1,0:T(8,128)(2,1)}, u32[]{:S(2)}) copy-start(bf16[3,1,128,64]{2,3,1,0:T(8,128)(2,1)} %param.32) | copy-start | bytes 147460
  18.3 24.8 %all-to-all-start.1 = ((bf16[8,64,512]{2,0,1:T(8,128)(2,1)}), bf16[8,64,512]{2,0,1:T(8,128)(2,1)S(1)}, u32[]{:S(2)}, u32[]{:S(2)}) async-start(bf16[8,64,512]{2,0,1:T(8,128)(2,1)} %copy.65), calls=%async_computation.1 | async-start | bytes 1048576 | tf_op jit(solution)/shard_map/all_to_all | solution.py:112
  31.6 1.5 copy-start.2
  43.0 70.2 %all-to-all-start = ((bf16[136,16,640]{2,0,1:T(8,128)(2,1)}), bf16[136,16,640]{2,0,1:T(8,128)(2,1)}, u32[]{:S(2)}, u32[]{:S(2)}) async-start(bf16[136,16,640]{2,0,1:T(8,128)(2,1)} %copy.63), calls=%async_computation | async-start | bytes 5570560 | tf_op jit(solution)/shard_map/all_to_all | solution.py:74
  50.1 54.4 %all-gather.5.cloned.1.call-start = ((), (), s32[]{:S(2)}) async-start(), calls=%async_computation.6 | async-start | bytes 2228224 | tf_op jit(solution)/shard_map/all_gather | solution.py:119
  52.4 79.7 %reduce-scatter.5.cloned.1.call-start = ((), (), s32[]{:S(2)}) async-start(), calls=%async_computation.7 | async-start | bytes 2752512 | tf_op jit(solution)/shard_map/reduce_scatter | solution.py:122
  117.4 56.9 %copy-start.5 = (bf16[64,448]{1,0:T(8,128)(2,1)S(1)}, bf16[64,448]{1,0:T(8,128)(2,1)}, u32[]{:S(2)}) copy-start(bf16[64,448]{1,0:T(8,128)(2,1)} %param.24) | copy-start | bytes 172036
  117.4 58.7 %copy-start.8 = (bf16[7168]{0:T(1024)(128)(2,1)S(1)}, bf16[7168]{0:T(1024)(128)(2,1)}, u32[]{:S(2)}) copy-start(bf16[7168]{0:T(1024)(128)(2,1)} %param.25) | copy-start | bytes 43012
  117.5 56.9 %reduce-scatter.7.cloned.1.call-start = ((), (), s32[]{:S(2)}) async-start(), calls=%async_computation.10 | async-start | bytes 1179648 | tf_op jit(solution)/shard_map/reduce_scatter | solution.py:123
  134.5 167.5 %all-gather.7.cloned.1.call-start = ((), (), s32[]{:S(2)}) async-start(), calls=%async_computation.8 | async-start | bytes 16842752 | tf_op jit(solution)/shard_map/all_gather | solution.py:133
  175.9 230.1 %all-gather.9.cloned.1.call-start = ((), (), s32[]{:S(2)}) async-start(), calls=%async_computation.9 | async-start | bytes 2785280 | tf_op jit(solution)/shard_map/all_gather | solution.py:148
  358.3 6.8 %copy-start.1 = (bf16[640,7168]{1,0:T(8,128)(2,1)S(1)}, bf16[640,7168]{1,0:T(8,128)(2,1)}, u32[]{:S(2)}) copy-start(bf16[640,7168]{1,0:T(8,128)(2,1)} %convert_element_type.97) | copy-start | bytes 27525124
  358.3 7.2 %copy-start.11 = (bf16[1,7168,128]{2,1,0:T(8,128)(2,1)S(1)}, bf16[1,7168,128]{2,1,0:T(8,128)(2,1)}, u32[]{:S(2)}) copy-start(bf16[1,7168,128]{2,1,0:T(8,128)(2,1)} %param.30) | copy-start | bytes 5505028
  410.4 3.4 copy-start.3
  417.2 34.4 %copy-start.9 = (f32[64,8]{0,1:T(8,128)S(1)}, f32[64,8]{0,1:T(8,128)}, u32[]{:S(2)}) copy-start(f32[64,8]{0,1:T(8,128)} %param.27) | copy-start | bytes 6148
  417.2 46.6 %copy-start.4 = (bf16[64,448]{1,0:T(8,128)(2,1)S(1)}, bf16[64,448]{1,0:T(8,128)(2,1)}, u32[]{:S(2)}) copy-start(bf16[64,448]{1,0:T(8,128)(2,1)} %add_convert_fusion) | copy-start | bytes 172036
  444.8 19.0 %all-to-all-start.3 = ((bf16[16,40,448]{2,1,0:T(8,128)(2,1)}), bf16[16,40,448]{2,1,0:T(8,128)(2,1)S(1)}, u32[]{:S(2)}, u32[]{:S(2)}) async-start(bf16[16,40,448]{2,1,0:T(8,128)(2,1)} %all_to_all.46), calls=%async_computation.4 | async-start | bytes 1310720 | tf_op jit(solution)/shard_map/all_to_all | solution.py:164
Sparse Core Ops, SparseCore 0:
  53.3 51.1 all-gather.4
  117.6 14.4 reduce-scatter.4
  134.7 39.6 reduce-scatter.6
  177.8 124.1 all-gather.6
  368.8 37.1 all-gather.8
